TPU v7x, 512 devices: a whole 4x4x16 slice. The times are simulated.
512 devices in a mesh: row: 16 (over z), col: 32 (over y, x, core).
Axes of the slice: x: 4, y: 4, z: 16, core: 2. Of those that a mesh axis runs over, the one named last changes fastest.
Arguments:
- inputs: bfloat16 [2048, 8192], P('col', 'row'), may hold values from -6 to 6
- gate_pre: bfloat16 [2048, 14784], P('row', 'col'), may hold values from -6 to 6
- up_pre: bfloat16 [2048, 14784], P('row', 'col'), may hold values from -6 to 6
- w_gate: bfloat16 [8192, 14784], P('row', 'col'), may hold values from -0.0625 to 0.0625
- w_up: bfloat16 [8192, 14784], P('row', 'col'), may hold values from -0.0625 to 0.0625
- w_down: bfloat16 [14784, 8192], P('col', 'row'), may hold values from -0.046875 to 0.046875
- grad_out: bfloat16 [2048, 8192], P('col', 'row'), may hold values from -1.5 to 1.5
Outputs:
- grad_in: bfloat16 [2048, 8192], P('col', 'row')
- grad_gate: bfloat16 [8192, 14784], P('row', 'col')
- grad_up: bfloat16 [8192, 14784], P('row', 'col')
- grad_down: bfloat16 [14784, 8192], P('col', 'row')
All inputs are finite; a program needn't handle non-finite values.
Results may differ from a plain program's by a relative error of at most 0.025.
Values may be sent and summed in bfloat16 or wider, within the bound.
No kernel may reach another device: no remote copies, remote signals or barrier semaphores. Data moves between devices by JAX's collectives and lax.ppermute only.
A program may use at most 64 MiB of HBM per device.

v0:
```python
import jax
import jax.numpy as jnp
from jax import lax
from jax.sharding import PartitionSpec as P


def contract_rows(left, right):
    return lax.dot_general(
        left, right, (((0,), (0,)), ((), ())), preferred_element_type=jnp.float32
    )


def contract_cols(left, right):
    return lax.dot_general(
        left, right, (((1,), (1,)), ((), ())), preferred_element_type=jnp.float32
    )


def pointwise(gate_pre, up_pre, hidden_grad):
    gate_value = gate_pre.astype(jnp.float32)
    up_value = up_pre.astype(jnp.float32)
    sigmoid_gate = jax.nn.sigmoid(gate_value)
    activated = gate_value * sigmoid_gate
    hidden = (activated * up_value).astype(jnp.bfloat16)
    up_grad = (hidden_grad * activated).astype(jnp.bfloat16)
    gate_grad = (
        hidden_grad * up_value * sigmoid_gate * (1.0 + gate_value * (1.0 - sigmoid_gate))
    ).astype(jnp.bfloat16)
    return (hidden, gate_grad, up_grad)


def _shifts(n):
    up = [(j, (j + 1) % n) for j in range(n)]
    down = [(j, (j - 1) % n) for j in range(n)]
    return (up, down)


def ring_all_gather(x, axis, n):
    me = lax.axis_index(axis)
    up, down = _shifts(n)
    n_up = n // 2
    n_down = n - 1 - n_up
    out = jnp.zeros((n,) + x.shape, x.dtype)
    out = lax.dynamic_update_index_in_dim(out, x, me, 0)
    a = x
    b = x
    for s in range(1, n_up + 1):
        a = lax.ppermute(a, axis, up)
        out = lax.dynamic_update_index_in_dim(out, a, (me - s + n) % n, 0)
        if s <= n_down:
            b = lax.ppermute(b, axis, down)
            out = lax.dynamic_update_index_in_dim(out, b, (me + s) % n, 0)
    return out


def ring_reduce_scatter(parts, axis, n, wire_dtype):
    me = lax.axis_index(axis)
    up, down = _shifts(n)
    n_up = n // 2
    n_down = n - 1 - n_up

    def block(j):
        return lax.dynamic_index_in_dim(parts, (j + 2 * n) % n, 0, keepdims=False).astype(
            jnp.float32
        )

    a = block(me + n_up)
    b = block(me - n_down)
    for s in range(n_up):
        a = lax.ppermute(a.astype(wire_dtype), axis, up).astype(jnp.float32)
        if s < n_up - 1:
            a = a + block(me + n_up - 1 - s)
        if s < n_down:
            b = lax.ppermute(b.astype(wire_dtype), axis, down).astype(jnp.float32)
            if s < n_down - 1:
                b = b + block(me - n_down + 1 + s)
    return block(me) + a + b


def shards(inputs, gate_pre, up_pre, w_gate, w_up, w_down, grad_out, n_row):
    tokens_row, hidden_units = gate_pre.shape
    pre = jnp.stack([gate_pre, up_pre], axis=1)
    all_pre = ring_all_gather(pre, "row", n_row).reshape((n_row * tokens_row, 2, hidden_units))
    all_grad_out = lax.all_gather(grad_out, "col", axis=0, tiled=True)
    all_inputs = lax.all_gather(inputs, "col", axis=0, tiled=True)
    part = contract_cols(all_grad_out, w_down).astype(jnp.bfloat16)
    part = part.reshape((n_row, tokens_row, hidden_units))
    own = ring_reduce_scatter(part, "row", n_row, jnp.bfloat16).astype(jnp.bfloat16)
    hidden_grad = ring_all_gather(own, "row", n_row).reshape((n_row * tokens_row, hidden_units))
    hidden, gate_grad, up_grad = pointwise(
        all_pre[:, 0], all_pre[:, 1], hidden_grad.astype(jnp.float32)
    )
    grad_down = contract_rows(hidden, all_grad_out).astype(jnp.bfloat16)
    grad_gate = contract_rows(all_inputs, gate_grad).astype(jnp.bfloat16)
    grad_up = contract_rows(all_inputs, up_grad).astype(jnp.bfloat16)
    grad_in = lax.psum_scatter(
        (contract_cols(gate_grad, w_gate) + contract_cols(up_grad, w_up)).astype(jnp.bfloat16),
        "col",
        scatter_dimension=0,
        tiled=True,
    )
    return (grad_in, grad_gate, grad_up, grad_down)


def solution(mesh):
    n_row = mesh.shape["row"]

    def body(*args):
        return shards(*args, n_row=n_row)

    return jax.shard_map(
        body,
        mesh=mesh,
        in_specs=(
            P("col", "row"),
            P("row", "col"),
            P("row", "col"),
            P("row", "col"),
            P("row", "col"),
            P("col", "row"),
            P("col", "row"),
        ),
        out_specs=(P("col", "row"), P("row", "col"), P("row", "col"), P("col", "row")),
        check_vma=False,
    )
```

profile of v0, /device:TPU:2, one launch (start us, length us, event | category | flops | bytes accessed | tf_op | source)
XLA Modules:
  0.0 708.0 jit_solution(4396758375819040371)
XLA Ops:
  9.0 3.8 collective-permute-start.30
  12.8 9.5 %collective-permute-start.31 = (bf16[128,2,462]{0,2,1:T(8,128)(2,1)S(1)}, bf16[128,2,462]{0,2,1:T(8,128)(2,1)}, u32[]{:S(2)}, u32[]{:S(2)}) collective-permute-start(bf16[128,2,462]{0,2,1:T(8,128)(2,1)S(1)} %get-tuple-element.22), channel_id=1, source_target_pairs={{0,480},{32,0},{64,32},{96,64},{128,96},{160,128},{192,160},{224,1... | collective-permute-start | bytes 709640 | tf_op jit(solution)/shard_map/ppermute | solution.py:51
  22.3 3.8 collective-permute-done.30
  28.3 5.1 collective-permute-start.33
  33.4 2.8 collective-permute-done.32
  38.2 36.0 %all-gather.3.cloned.1.call-done = bf16[2048,512]{1,0:T(8,128)(2,1)} async-done(((bf16[64,512]{1,0:T(8,128)(2,1)}), bf16[2048,512]{1,0:T(8,128)(2,1)}) %all-gather.3.cloned.1.call-update) | async-done | bytes 2097168 | tf_op jit(solution)/shard_map/all_gather | solution.py:84
  74.2 2.8 convolution_convert_fusion
  77.9 4.8 constant_dynamic-slice_fusion.15
  82.7 3.5 collective-permute-start
  86.3 4.4 collective-permute-start.35
  92.6 5.1 collective-permute-start.8
  101.7 5.1 collective-permute-start.9
  110.8 5.1 collective-permute-start.10
  118.3 5.5 collective-permute-start.11
  126.3 5.5 collective-permute-start.12
  134.3 5.5 collective-permute-start.13
  142.3 5.6 collective-permute-start.14
  150.0 5.1 collective-permute-start.37
  159.5 4.9 collective-permute-start.16
  168.0 5.1 collective-permute-start.39
  175.1 5.1 collective-permute-start.18
  182.6 5.6 collective-permute-start.20
  190.2 5.1 collective-permute-start.41
  197.3 5.1 collective-permute-start.22
  204.8 5.5 collective-permute-start.24
  212.3 5.1 collective-permute-start.43
  219.4 5.1 collective-permute-start.26
  226.9 5.6 collective-permute-start.28
  237.7 14.5 %dynamic_update_slice.114 = bf16[16,128,2,462]{1,0,3,2:T(8,128)(2,1)} dynamic-update-slice(bf16[16,128,2,462]{1,0,3,2:T(8,128)(2,1)} %broadcast_in_dim.121, bf16[1,128,2,462]{1,0,3,2:T(2,128)(2,1)S(1)} %copy.56, s32[]{:T(128)S(6)} %select_n.304, s32[]{:T(128)} %constant.338.clone.1, s32[]{:T(128)} %constant.338.clone.1, s32[]{:T(128)} %constant.338.clone.1) | dynamic-update-slice | bytes 473092 | tf_op jit(solution)/shard_map/jit(dynamic_update_index_in_dim)/dynamic_update_slice | solution.py:44
  253.8 14.3 %dynamic_update_slice.115 = bf16[16,128,2,462]{1,0,3,2:T(8,128)(2,1)} dynamic-update-slice(bf16[16,128,2,462]{1,0,3,2:T(8,128)(2,1)} %dynamic_update_slice.114, bf16[1,128,2,462]{1,0,3,2:T(2,128)(2,1)S(1)} %copy.57, s32[]{:T(128)S(6)} %select_n.306, s32[]{:T(128)} %constant.338.clone.1, s32[]{:T(128)} %constant.338.clone.1, s32[]{:T(128)} %constant.338.clone.1) | dynamic-update-slice | bytes 473092 | tf_op jit(solution)/shard_map/jit(dynamic_update_index_in_dim)/dynamic_update_slice | solution.py:49
  268.1 14.3 %dynamic_update_slice.116 = bf16[16,128,2,462]{1,0,3,2:T(8,128)(2,1)} dynamic-update-slice(bf16[16,128,2,462]{1,0,3,2:T(8,128)(2,1)} %dynamic_update_slice.115, bf16[1,128,2,462]{1,0,3,2:T(2,128)(2,1)S(1)} %copy.58, s32[]{:T(128)S(6)} %select_n.308, s32[]{:T(128)} %constant.338.clone.1, s32[]{:T(128)} %constant.338.clone.1, s32[]{:T(128)} %constant.338.clone.1) | dynamic-update-slice | bytes 473092 | tf_op jit(solution)/shard_map/jit(dynamic_update_index_in_dim)/dynamic_update_slice | solution.py:52
  285.1 14.3 %dynamic_update_slice.117 = bf16[16,128,2,462]{1,0,3,2:T(8,128)(2,1)} dynamic-update-slice(bf16[16,128,2,462]{1,0,3,2:T(8,128)(2,1)} %dynamic_update_slice.116, bf16[1,128,2,462]{1,0,3,2:T(2,128)(2,1)S(1)} %copy.59, s32[]{:T(128)S(6)} %select_n.310, s32[]{:T(128)} %constant.338.clone.1, s32[]{:T(128)} %constant.338.clone.1, s32[]{:T(128)} %constant.338.clone.1) | dynamic-update-slice | bytes 473092 | tf_op jit(solution)/shard_map/jit(dynamic_update_index_in_dim)/dynamic_update_slice | solution.py:49
  299.4 14.3 %dynamic_update_slice.118 = bf16[16,128,2,462]{1,0,3,2:T(8,128)(2,1)} dynamic-update-slice(bf16[16,128,2,462]{1,0,3,2:T(8,128)(2,1)} %dynamic_update_slice.117, bf16[1,128,2,462]{1,0,3,2:T(2,128)(2,1)S(1)} %copy.60, s32[]{:T(128)S(6)} %select_n.312, s32[]{:T(128)} %constant.338.clone.1, s32[]{:T(128)} %constant.338.clone.1, s32[]{:T(128)} %constant.338.clone.1) | dynamic-update-slice | bytes 473092 | tf_op jit(solution)/shard_map/jit(dynamic_update_index_in_dim)/dynamic_update_slice | solution.py:52
  315.4 14.3 %dynamic_update_slice.119 = bf16[16,128,2,462]{1,0,3,2:T(8,128)(2,1)} dynamic-update-slice(bf16[16,128,2,462]{1,0,3,2:T(8,128)(2,1)} %dynamic_update_slice.118, bf16[1,128,2,462]{1,0,3,2:T(2,128)(2,1)S(1)} %copy.61, s32[]{:T(128)S(6)} %select_n.314, s32[]{:T(128)} %constant.338.clone.1, s32[]{:T(128)} %constant.338.clone.1, s32[]{:T(128)} %constant.338.clone.1) | dynamic-update-slice | bytes 473092 | tf_op jit(solution)/shard_map/jit(dynamic_update_index_in_dim)/dynamic_update_slice | solution.py:49
  329.7 14.3 %dynamic_update_slice.120 = bf16[16,128,2,462]{1,0,3,2:T(8,128)(2,1)} dynamic-update-slice(bf16[16,128,2,462]{1,0,3,2:T(8,128)(2,1)} %dynamic_update_slice.119, bf16[1,128,2,462]{1,0,3,2:T(2,128)(2,1)S(1)} %copy.62, s32[]{:T(128)S(6)} %select_n.316, s32[]{:T(128)} %constant.338.clone.1, s32[]{:T(128)} %constant.338.clone.1, s32[]{:T(128)} %constant.338.clone.1) | dynamic-update-slice | bytes 473092 | tf_op jit(solution)/shard_map/jit(dynamic_update_index_in_dim)/dynamic_update_slice | solution.py:52
  344.7 14.3 %dynamic_update_slice.121 = bf16[16,128,2,462]{1,0,3,2:T(8,128)(2,1)} dynamic-update-slice(bf16[16,128,2,462]{1,0,3,2:T(8,128)(2,1)} %dynamic_update_slice.120, bf16[1,128,2,462]{1,0,3,2:T(2,128)(2,1)S(1)} %copy.63, s32[]{:T(128)S(6)} %select_n.318, s32[]{:T(128)} %constant.338.clone.1, s32[]{:T(128)} %constant.338.clone.1, s32[]{:T(128)} %constant.338.clone.1) | dynamic-update-slice | bytes 473092 | tf_op jit(solution)/shard_map/jit(dynamic_update_index_in_dim)/dynamic_update_slice | solution.py:49
  359.0 14.3 %dynamic_update_slice.122 = bf16[16,128,2,462]{1,0,3,2:T(8,128)(2,1)} dynamic-update-slice(bf16[16,128,2,462]{1,0,3,2:T(8,128)(2,1)} %dynamic_update_slice.121, bf16[1,128,2,462]{1,0,3,2:T(2,128)(2,1)S(1)} %copy.64, s32[]{:T(128)S(6)} %select_n.320, s32[]{:T(128)} %constant.338.clone.1, s32[]{:T(128)} %constant.338.clone.1, s32[]{:T(128)} %constant.338.clone.1) | dynamic-update-slice | bytes 473092 | tf_op jit(solution)/shard_map/jit(dynamic_update_index_in_dim)/dynamic_update_slice | solution.py:52
  374.0 14.3 %dynamic_update_slice.123 = bf16[16,128,2,462]{1,0,3,2:T(8,128)(2,1)} dynamic-update-slice(bf16[16,128,2,462]{1,0,3,2:T(8,128)(2,1)} %dynamic_update_slice.122, bf16[1,128,2,462]{1,0,3,2:T(2,128)(2,1)S(1)} %copy.65, s32[]{:T(128)S(6)} %select_n.322, s32[]{:T(128)} %constant.338.clone.1, s32[]{:T(128)} %constant.338.clone.1, s32[]{:T(128)} %constant.338.clone.1) | dynamic-update-slice | bytes 473092 | tf_op jit(solution)/shard_map/jit(dynamic_update_index_in_dim)/dynamic_update_slice | solution.py:49
  388.3 14.3 %dynamic_update_slice.124 = bf16[16,128,2,462]{1,0,3,2:T(8,128)(2,1)} dynamic-update-slice(bf16[16,128,2,462]{1,0,3,2:T(8,128)(2,1)} %dynamic_update_slice.123, bf16[1,128,2,462]{1,0,3,2:T(2,128)(2,1)S(1)} %copy.66, s32[]{:T(128)S(6)} %select_n.324, s32[]{:T(128)} %constant.338.clone.1, s32[]{:T(128)} %constant.338.clone.1, s32[]{:T(128)} %constant.338.clone.1) | dynamic-update-slice | bytes 473092 | tf_op jit(solution)/shard_map/jit(dynamic_update_index_in_dim)/dynamic_update_slice | solution.py:52
  403.3 14.5 %dynamic_update_slice.125 = bf16[16,128,2,462]{1,0,3,2:T(8,128)(2,1)} dynamic-update-slice(bf16[16,128,2,462]{1,0,3,2:T(8,128)(2,1)} %dynamic_update_slice.124, bf16[1,128,2,462]{1,0,3,2:T(2,128)(2,1)S(1)} %copy.67, s32[]{:T(128)S(6)} %select_n.326, s32[]{:T(128)} %constant.338.clone.1, s32[]{:T(128)} %constant.338.clone.1, s32[]{:T(128)} %constant.338.clone.1) | dynamic-update-slice | bytes 473092 | tf_op jit(solution)/shard_map/jit(dynamic_update_index_in_dim)/dynamic_update_slice | solution.py:49
  417.9 14.3 %dynamic_update_slice.126 = bf16[16,128,2,462]{1,0,3,2:T(8,128)(2,1)} dynamic-update-slice(bf16[16,128,2,462]{1,0,3,2:T(8,128)(2,1)} %dynamic_update_slice.125, bf16[1,128,2,462]{1,0,3,2:T(2,128)(2,1)S(1)} %copy.68, s32[]{:T(128)S(6)} %select_n.328, s32[]{:T(128)} %constant.338.clone.1, s32[]{:T(128)} %constant.338.clone.1, s32[]{:T(128)} %constant.338.clone.1) | dynamic-update-slice | bytes 473092 | tf_op jit(solution)/shard_map/jit(dynamic_update_index_in_dim)/dynamic_update_slice | solution.py:52
  433.8 14.3 %dynamic_update_slice.127 = bf16[16,128,2,462]{1,0,3,2:T(8,128)(2,1)} dynamic-update-slice(bf16[16,128,2,462]{1,0,3,2:T(8,128)(2,1)} %dynamic_update_slice.126, bf16[1,128,2,462]{1,0,3,2:T(2,128)(2,1)S(1)} %copy.69, s32[]{:T(128)S(6)} %select_n.330, s32[]{:T(128)} %constant.338.clone.1, s32[]{:T(128)} %constant.338.clone.1, s32[]{:T(128)} %constant.338.clone.1) | dynamic-update-slice | bytes 473092 | tf_op jit(solution)/shard_map/jit(dynamic_update_index_in_dim)/dynamic_update_slice | solution.py:49
  448.1 14.3 %dynamic_update_slice.128 = bf16[16,128,2,462]{1,0,3,2:T(8,128)(2,1)} dynamic-update-slice(bf16[16,128,2,462]{1,0,3,2:T(8,128)(2,1)} %dynamic_update_slice.127, bf16[1,128,2,462]{1,0,3,2:T(2,128)(2,1)S(1)} %copy.70, s32[]{:T(128)S(6)} %select_n.332, s32[]{:T(128)} %constant.338.clone.1, s32[]{:T(128)} %constant.338.clone.1, s32[]{:T(128)} %constant.338.clone.1) | dynamic-update-slice | bytes 473092 | tf_op jit(solution)/shard_map/jit(dynamic_update_index_in_dim)/dynamic_update_slice | solution.py:52
  463.7 14.3 %dynamic_update_slice.129 = bf16[16,128,2,462]{1,0,3,2:T(8,128)(2,1)} dynamic-update-slice(bf16[16,128,2,462]{1,0,3,2:T(8,128)(2,1)} %dynamic_update_slice.128, bf16[1,128,2,462]{1,0,3,2:T(2,128)(2,1)S(1)} %copy.71, s32[]{:T(128)S(6)} %select_n.334, s32[]{:T(128)} %constant.338.clone.1, s32[]{:T(128)} %constant.338.clone.1, s32[]{:T(128)} %constant.338.clone.1) | dynamic-update-slice | bytes 473092 | tf_op jit(solution)/shard_map/jit(dynamic_update_index_in_dim)/dynamic_update_slice | solution.py:49
  478.0 4.5 reshape.50
  483.0 6.2 dynamic_update_slice.98
  489.6 6.2 dynamic_update_slice.99
  495.7 6.2 dynamic_update_slice.100
  502.3 6.2 dynamic_update_slice.101
  508.5 6.2 dynamic_update_slice.102
  515.0 6.2 dynamic_update_slice.103
  521.2 6.2 dynamic_update_slice.104
  527.8 6.6 dynamic_update_slice.105
  534.3 6.2 dynamic_update_slice.106
  540.9 6.2 dynamic_update_slice.107
  547.0 6.2 dynamic_update_slice.108
  554.5 6.2 dynamic_update_slice.109
  560.7 6.2 dynamic_update_slice.110
  569.0 6.2 dynamic_update_slice.111
  575.2 6.2 dynamic_update_slice.112
  582.4 6.2 dynamic_update_slice.113
  597.5 4.7 fusion.10
  602.3 3.7 fusion.13
  607.8 93.5 %reduce-scatter.2.cloned.1.call-done = bf16[64,512]{1,0:T(8,128)(2,1)} async-done(((bf16[2048,512]{1,0:T(8,128)(2,1)}), bf16[64,512]{1,0:T(8,128)(2,1)}) %reduce-scatter.2.cloned.1.call-update) | async-done | bytes 65552 | tf_op jit(solution)/shard_map/reduce_scatter | solution.py:96
  (200 shorter events, 86.1 us)
Async XLA Ops:
  7.2 586.2 %copy-start = (bf16[512,462]{0,1:T(8,128)(2,1)S(1)}, bf16[512,462]{0,1:T(8,128)(2,1)}, u32[]{:S(2)}) copy-start(bf16[512,462]{0,1:T(8,128)(2,1)} %param.10) | copy-start | bytes 1419268
  7.2 67.0 %all-gather.3.cloned.1.call-start = ((), (), s32[]{:S(2)}) async-start(), calls=%async_computation.1 | async-start | bytes 2162688 | tf_op jit(solution)/shard_map/all_gather | solution.py:84
  7.9 594.3 %all-gather.5.cloned.1.call-start = ((), (), s32[]{:S(2)}) async-start(), calls=%async_computation.3 | async-start | bytes 2162688 | tf_op jit(solution)/shard_map/all_gather | solution.py:85
  9.0 17.2 %collective-permute-start.30 = (bf16[128,2,462]{0,2,1:T(8,128)(2,1)S(1)}, bf16[128,2,462]{0,2,1:T(8,128)(2,1)S(1)}, u32[]{:S(2)}, u32[]{:S(2)}) collective-permute-start(bf16[128,2,462]{0,2,1:T(8,128)(2,1)S(1)} %get-tuple-element.22), channel_id=1, source_target_pairs={{0,32},{32,64},{64,96},{96,128},{128,160},{160,192},{192,224},{224... | collective-permute-start | bytes 709640 | tf_op jit(solution)/shard_map/ppermute | solution.py:48
  12.8 15.5 %collective-permute-start.31 = (bf16[128,2,462]{0,2,1:T(8,128)(2,1)S(1)}, bf16[128,2,462]{0,2,1:T(8,128)(2,1)}, u32[]{:S(2)}, u32[]{:S(2)}) collective-permute-start(bf16[128,2,462]{0,2,1:T(8,128)(2,1)S(1)} %get-tuple-element.22), channel_id=1, source_target_pairs={{0,480},{32,0},{64,32},{96,64},{128,96},{160,128},{192,160},{224,1... | collective-permute-start | bytes 709640 | tf_op jit(solution)/shard_map/ppermute | solution.py:51
  26.1 50.9 %copy-start.5 = (bf16[128,2,462]{0,2,1:T(8,128)(2,1)}, bf16[128,2,462]{0,2,1:T(8,128)(2,1)S(1)}, u32[]{:S(2)}) copy-start(bf16[128,2,462]{0,2,1:T(8,128)(2,1)S(1)} %collective-permute-done.30) | copy-start | bytes 709636
  26.1 10.1 %collective-permute-start.32 = (bf16[128,2,462]{0,2,1:T(8,128)(2,1)S(1)}, bf16[128,2,462]{0,2,1:T(8,128)(2,1)}, u32[]{:S(2)}, u32[]{:S(2)}) collective-permute-start(bf16[128,2,462]{0,2,1:T(8,128)(2,1)S(1)} %collective-permute-done.30), channel_id=1, source_target_pairs={{0,32},{32,64},{64,96},{96,128},{128,160},{160,192},{192,224},{224... | collective-permute-start | bytes 709640 | tf_op jit(solution)/shard_map/ppermute | solution.py:48
  28.3 58.0 %collective-permute-start.33 = (bf16[128,2,462]{0,2,1:T(8,128)(2,1)}, bf16[128,2,462]{0,2,1:T(8,128)(2,1)}, u32[]{:S(2)}, u32[]{:S(2)}) collective-permute-start(bf16[128,2,462]{0,2,1:T(8,128)(2,1)} %collective-permute-done.31), channel_id=1, source_target_pairs={{0,480},{32,0},{64,32},{96,64},{128,96},{160,128},{192,160},{224,1... | collective-permute-start | bytes 709640 | tf_op jit(solution)/shard_map/ppermute | solution.py:51
  36.3 54.4 %collective-permute-start.34 = (bf16[128,2,462]{0,2,1:T(8,128)(2,1)}, bf16[128,2,462]{0,2,1:T(8,128)(2,1)}, u32[]{:S(2)}, u32[]{:S(2)}) collective-permute-start(bf16[128,2,462]{0,2,1:T(8,128)(2,1)} %collective-permute-done.32), channel_id=1, source_target_pairs={{0,32},{32,64},{64,96},{96,128},{128,160},{160,192},{192,224},{224... | collective-permute-start | bytes 709640 | tf_op jit(solution)/shard_map/ppermute | solution.py:48
  82.7 15.1 %collective-permute-start = (bf16[128,462]{0,1:T(8,128)(2,1)S(1)}, bf16[128,462]{0,1:T(8,128)(2,1)}, u32[]{:S(2)}, u32[]{:S(2)}) collective-permute-start(bf16[128,462]{0,1:T(8,128)(2,1)S(1)} %bitcast.191), channel_id=1, source_target_pairs={{0,32},{32,64},{64,96},{96,128},{128,160},{160,192},{192,224},{224... | collective-permute-start | bytes 354824 | tf_op jit(solution)/shard_map/ppermute | solution.py:70
  86.2 615.1 %reduce-scatter.2.cloned.1.call-start = ((), (), s32[]{:S(2)}) async-start(), calls=%async_computation.2 | async-start | bytes 2162688 | tf_op jit(solution)/shard_map/reduce_scatter | solution.py:96
  86.3 63.7 %collective-permute-start.35 = (bf16[128,2,462]{0,2,1:T(8,128)(2,1)}, bf16[128,2,462]{0,2,1:T(8,128)(2,1)S(1)}, u32[]{:S(2)}, u32[]{:S(2)}) collective-permute-start(bf16[128,2,462]{0,2,1:T(8,128)(2,1)} %collective-permute-done.33), channel_id=1, source_target_pairs={{0,480},{32,0},{64,32},{96,64},{128,96},{160,128},{192,160},{224,1... | collective-permute-start | bytes 709640 | tf_op jit(solution)/shard_map/ppermute | solution.py:51
  90.7 64.4 %collective-permute-start.36 = (bf16[128,2,462]{0,2,1:T(8,128)(2,1)}, bf16[128,2,462]{0,2,1:T(8,128)(2,1)S(1)}, u32[]{:S(2)}, u32[]{:S(2)}) collective-permute-start(bf16[128,2,462]{0,2,1:T(8,128)(2,1)} %collective-permute-done.34), channel_id=1, source_target_pairs={{0,32},{32,64},{64,96},{96,128},{128,160},{160,192},{192,224},{224... | collective-permute-start | bytes 709640 | tf_op jit(solution)/shard_map/ppermute | solution.py:48
  92.6 8.1 %collective-permute-start.8 = (bf16[128,462]{0,1:T(8,128)(2,1)S(1)}, bf16[128,462]{0,1:T(8,128)(2,1)S(1)}, u32[]{:S(2)}, u32[]{:S(2)}) collective-permute-start(bf16[128,462]{0,1:T(8,128)(2,1)S(1)} %bitcast.192), channel_id=1, source_target_pairs={{0,480},{32,0},{64,32},{96,64},{128,96},{160,128},{192,160},{224,1... | collective-permute-start | bytes 354824 | tf_op jit(solution)/shard_map/ppermute | solution.py:74
  98.8 8.1 %collective-permute-start.1 = (bf16[128,462]{0,1:T(8,128)(2,1)S(1)}, bf16[128,462]{0,1:T(8,128)(2,1)S(1)}, u32[]{:S(2)}, u32[]{:S(2)}) collective-permute-start(bf16[128,462]{0,1:T(8,128)(2,1)S(1)} %fusion.27), channel_id=1, source_target_pairs={{0,32},{32,64},{64,96},{96,128},{128,160},{160,192},{192,224},{224... | collective-permute-start | bytes 354824 | tf_op jit(solution)/shard_map/ppermute | solution.py:70
  101.7 8.1 %collective-permute-start.9 = (bf16[128,462]{0,1:T(8,128)(2,1)S(1)}, bf16[128,462]{0,1:T(8,128)(2,1)S(1)}, u32[]{:S(2)}, u32[]{:S(2)}) collective-permute-start(bf16[128,462]{0,1:T(8,128)(2,1)S(1)} %fusion.20), channel_id=1, source_target_pairs={{0,480},{32,0},{64,32},{96,64},{128,96},{160,128},{192,160},{224,1... | collective-permute-start | bytes 354824 | tf_op jit(solution)/shard_map/ppermute | solution.py:74
  107.9 8.1 %collective-permute-start.2 = (bf16[128,462]{0,1:T(8,128)(2,1)S(1)}, bf16[128,462]{0,1:T(8,128)(2,1)S(1)}, u32[]{:S(2)}, u32[]{:S(2)}) collective-permute-start(bf16[128,462]{0,1:T(8,128)(2,1)S(1)} %fusion.26), channel_id=1, source_target_pairs={{0,32},{32,64},{64,96},{96,128},{128,160},{160,192},{192,224},{224... | collective-permute-start | bytes 354824 | tf_op jit(solution)/shard_map/ppermute | solution.py:70
  110.8 7.5 %collective-permute-start.10 = (bf16[128,462]{0,1:T(8,128)(2,1)S(1)}, bf16[128,462]{0,1:T(8,128)(2,1)S(1)}, u32[]{:S(2)}, u32[]{:S(2)}) collective-permute-start(bf16[128,462]{0,1:T(8,128)(2,1)S(1)} %fusion.19), channel_id=1, source_target_pairs={{0,480},{32,0},{64,32},{96,64},{128,96},{160,128},{192,160},{224,1... | collective-permute-start | bytes 354824 | tf_op jit(solution)/shard_map/ppermute | solution.py:74
  116.0 7.9 %collective-permute-start.3 = (bf16[128,462]{0,1:T(8,128)(2,1)S(1)}, bf16[128,462]{0,1:T(8,128)(2,1)S(1)}, u32[]{:S(2)}, u32[]{:S(2)}) collective-permute-start(bf16[128,462]{0,1:T(8,128)(2,1)S(1)} %fusion.25), channel_id=1, source_target_pairs={{0,32},{32,64},{64,96},{96,128},{128,160},{160,192},{192,224},{224... | collective-permute-start | bytes 354824 | tf_op jit(solution)/shard_map/ppermute | solution.py:70
  118.3 7.9 %collective-permute-start.11 = (bf16[128,462]{0,1:T(8,128)(2,1)S(1)}, bf16[128,462]{0,1:T(8,128)(2,1)S(1)}, u32[]{:S(2)}, u32[]{:S(2)}) collective-permute-start(bf16[128,462]{0,1:T(8,128)(2,1)S(1)} %fusion.18), channel_id=1, source_target_pairs={{0,480},{32,0},{64,32},{96,64},{128,96},{160,128},{192,160},{224,1... | collective-permute-start | bytes 354824 | tf_op jit(solution)/shard_map/ppermute | solution.py:74
  124.0 7.9 %collective-permute-start.4 = (bf16[128,462]{0,1:T(8,128)(2,1)S(1)}, bf16[128,462]{0,1:T(8,128)(2,1)S(1)}, u32[]{:S(2)}, u32[]{:S(2)}) collective-permute-start(bf16[128,462]{0,1:T(8,128)(2,1)S(1)} %fusion.24), channel_id=1, source_target_pairs={{0,32},{32,64},{64,96},{96,128},{128,160},{160,192},{192,224},{224... | collective-permute-start | bytes 354824 | tf_op jit(solution)/shard_map/ppermute | solution.py:70
  126.3 7.9 %collective-permute-start.12 = (bf16[128,462]{0,1:T(8,128)(2,1)S(1)}, bf16[128,462]{0,1:T(8,128)(2,1)S(1)}, u32[]{:S(2)}, u32[]{:S(2)}) collective-permute-start(bf16[128,462]{0,1:T(8,128)(2,1)S(1)} %fusion.17), channel_id=1, source_target_pairs={{0,480},{32,0},{64,32},{96,64},{128,96},{160,128},{192,160},{224,1... | collective-permute-start | bytes 354824 | tf_op jit(solution)/shard_map/ppermute | solution.py:74
  131.9 7.9 %collective-permute-start.5 = (bf16[128,462]{0,1:T(8,128)(2,1)S(1)}, bf16[128,462]{0,1:T(8,128)(2,1)S(1)}, u32[]{:S(2)}, u32[]{:S(2)}) collective-permute-start(bf16[128,462]{0,1:T(8,128)(2,1)S(1)} %fusion.23), channel_id=1, source_target_pairs={{0,32},{32,64},{64,96},{96,128},{128,160},{160,192},{192,224},{224... | collective-permute-start | bytes 354824 | tf_op jit(solution)/shard_map/ppermute | solution.py:70
  134.3 8.0 %collective-permute-start.13 = (bf16[128,462]{0,1:T(8,128)(2,1)S(1)}, bf16[128,462]{0,1:T(8,128)(2,1)S(1)}, u32[]{:S(2)}, u32[]{:S(2)}) collective-permute-start(bf16[128,462]{0,1:T(8,128)(2,1)S(1)} %fusion.16), channel_id=1, source_target_pairs={{0,480},{32,0},{64,32},{96,64},{128,96},{160,128},{192,160},{224,1... | collective-permute-start | bytes 354824 | tf_op jit(solution)/shard_map/ppermute | solution.py:74
  139.9 8.0 %collective-permute-start.6 = (bf16[128,462]{0,1:T(8,128)(2,1)S(1)}, bf16[128,462]{0,1:T(8,128)(2,1)S(1)}, u32[]{:S(2)}, u32[]{:S(2)}) collective-permute-start(bf16[128,462]{0,1:T(8,128)(2,1)S(1)} %fusion.22), channel_id=1, source_target_pairs={{0,32},{32,64},{64,96},{96,128},{128,160},{160,192},{192,224},{224... | collective-permute-start | bytes 354824 | tf_op jit(solution)/shard_map/ppermute | solution.py:70
  142.3 14.7 %collective-permute-start.14 = (bf16[128,462]{0,1:T(8,128)(2,1)S(1)}, bf16[128,462]{0,1:T(8,128)(2,1)S(1)}, u32[]{:S(2)}, u32[]{:S(2)}) collective-permute-start(bf16[128,462]{0,1:T(8,128)(2,1)S(1)} %fusion.15), channel_id=1, source_target_pairs={{0,480},{32,0},{64,32},{96,64},{128,96},{160,128},{192,160},{224,1... | collective-permute-start | bytes 354824 | tf_op jit(solution)/shard_map/ppermute | solution.py:74
  148.0 9.2 %collective-permute-start.7 = (bf16[128,462]{0,1:T(8,128)(2,1)S(1)}, bf16[128,462]{0,1:T(8,128)(2,1)S(1)}, u32[]{:S(2)}, u32[]{:S(2)}) collective-permute-start(bf16[128,462]{0,1:T(8,128)(2,1)S(1)} %fusion.21), channel_id=1, source_target_pairs={{0,32},{32,64},{64,96},{96,128},{128,160},{160,192},{192,224},{224... | collective-permute-start | bytes 354824 | tf_op jit(solution)/shard_map/ppermute | solution.py:70
  150.0 18.0 %collective-permute-start.37 = (bf16[128,2,462]{0,2,1:T(8,128)(2,1)S(1)}, bf16[128,2,462]{0,2,1:T(8,128)(2,1)S(1)}, u32[]{:S(2)}, u32[]{:S(2)}) collective-permute-start(bf16[128,2,462]{0,2,1:T(8,128)(2,1)S(1)} %collective-permute-done.35), channel_id=1, source_target_pairs={{0,480},{32,0},{64,32},{96,64},{128,96},{160,128},{192,160},{224,1... | collective-permute-start | bytes 709640 | tf_op jit(solution)/shard_map/ppermute | solution.py:51
  155.1 18.0 %collective-permute-start.38 = (bf16[128,2,462]{0,2,1:T(8,128)(2,1)S(1)}, bf16[128,2,462]{0,2,1:T(8,128)(2,1)S(1)}, u32[]{:S(2)}, u32[]{:S(2)}) collective-permute-start(bf16[128,2,462]{0,2,1:T(8,128)(2,1)S(1)} %collective-permute-done.36), channel_id=1, source_target_pairs={{0,32},{32,64},{64,96},{96,128},{128,160},{160,192},{192,224},{224... | collective-permute-start | bytes 709640 | tf_op jit(solution)/shard_map/ppermute | solution.py:48
  157.3 8.8 %collective-permute-start.15 = (bf16[128,462]{0,1:T(8,128)(2,1)S(1)}, bf16[128,462]{0,1:T(8,128)(2,1)S(1)}, u32[]{:S(2)}, u32[]{:S(2)}) collective-permute-start(bf16[128,462]{0,1:T(8,128)(2,1)S(1)} %fusion.29), channel_id=1, source_target_pairs={{0,32},{32,64},{64,96},{96,128},{128,160},{160,192},{192,224},{224... | collective-permute-start | bytes 354824 | tf_op jit(solution)/shard_map/ppermute | solution.py:48
  159.5 15.6 %collective-permute-start.16 = (bf16[128,462]{0,1:T(8,128)(2,1)S(1)}, bf16[128,462]{0,1:T(8,128)(2,1)S(1)}, u32[]{:S(2)}, u32[]{:S(2)}) collective-permute-start(bf16[128,462]{0,1:T(8,128)(2,1)S(1)} %fusion.29), channel_id=1, source_target_pairs={{0,480},{32,0},{64,32},{96,64},{128,96},{160,128},{192,160},{224,1... | collective-permute-start | bytes 354824 | tf_op jit(solution)/shard_map/ppermute | solution.py:51
  166.0 71.6 %copy-start.13 = (bf16[128,462]{0,1:T(8,128)(2,1)}, bf16[128,462]{0,1:T(8,128)(2,1)S(1)}, u32[]{:S(2)}) copy-start(bf16[128,462]{0,1:T(8,128)(2,1)S(1)} %collective-permute-done.15) | copy-start | bytes 354820
  166.0 14.2 %collective-permute-start.17 = (bf16[128,462]{0,1:T(8,128)(2,1)S(1)}, bf16[128,462]{0,1:T(8,128)(2,1)S(1)}, u32[]{:S(2)}, u32[]{:S(2)}) collective-permute-start(bf16[128,462]{0,1:T(8,128)(2,1)S(1)} %collective-permute-done.15), channel_id=1, source_target_pairs={{0,32},{32,64},{64,96},{96,128},{128,160},{160,192},{192,224},{224... | collective-permute-start | bytes 354824 | tf_op jit(solution)/shard_map/ppermute | solution.py:48
  168.0 22.2 %collective-permute-start.39 = (bf16[128,2,462]{0,2,1:T(8,128)(2,1)S(1)}, bf16[128,2,462]{0,2,1:T(8,128)(2,1)S(1)}, u32[]{:S(2)}, u32[]{:S(2)}) collective-permute-start(bf16[128,2,462]{0,2,1:T(8,128)(2,1)S(1)} %collective-permute-done.37), channel_id=1, source_target_pairs={{0,480},{32,0},{64,32},{96,64},{128,96},{160,128},{192,160},{224,1... | collective-permute-start | bytes 709640 | tf_op jit(solution)/shard_map/ppermute | solution.py:51
  173.1 22.2 %collective-permute-start.40 = (bf16[128,2,462]{0,2,1:T(8,128)(2,1)S(1)}, bf16[128,2,462]{0,2,1:T(8,128)(2,1)S(1)}, u32[]{:S(2)}, u32[]{:S(2)}) collective-permute-start(bf16[128,2,462]{0,2,1:T(8,128)(2,1)S(1)} %collective-permute-done.38), channel_id=1, source_target_pairs={{0,32},{32,64},{64,96},{96,128},{128,160},{160,192},{192,224},{224... | collective-permute-start | bytes 709640 | tf_op jit(solution)/shard_map/ppermute | solution.py:48
  175.1 62.6 %copy-start.15 = (bf16[128,462]{0,1:T(8,128)(2,1)}, bf16[128,462]{0,1:T(8,128)(2,1)S(1)}, u32[]{:S(2)}) copy-start(bf16[128,462]{0,1:T(8,128)(2,1)S(1)} %collective-permute-done.16) | copy-start | bytes 354820
  175.1 7.5 %collective-permute-start.18 = (bf16[128,462]{0,1:T(8,128)(2,1)S(1)}, bf16[128,462]{0,1:T(8,128)(2,1)S(1)}, u32[]{:S(2)}, u32[]{:S(2)}) collective-permute-start(bf16[128,462]{0,1:T(8,128)(2,1)S(1)} %collective-permute-done.16), channel_id=1, source_target_pairs={{0,480},{32,0},{64,32},{96,64},{128,96},{160,128},{192,160},{224,1... | collective-permute-start | bytes 354824 | tf_op jit(solution)/shard_map/ppermute | solution.py:51
  180.2 57.4 %copy-start.11 = (bf16[128,462]{0,1:T(8,128)(2,1)}, bf16[128,462]{0,1:T(8,128)(2,1)S(1)}, u32[]{:S(2)}) copy-start(bf16[128,462]{0,1:T(8,128)(2,1)S(1)} %collective-permute-done.17) | copy-start | bytes 354820
  180.2 8.0 %collective-permute-start.19 = (bf16[128,462]{0,1:T(8,128)(2,1)S(1)}, bf16[128,462]{0,1:T(8,128)(2,1)S(1)}, u32[]{:S(2)}, u32[]{:S(2)}) collective-permute-start(bf16[128,462]{0,1:T(8,128)(2,1)S(1)} %collective-permute-done.17), channel_id=1, source_target_pairs={{0,32},{32,64},{64,96},{96,128},{128,160},{160,192},{192,224},{224... | collective-permute-start | bytes 354824 | tf_op jit(solution)/shard_map/ppermute | solution.py:48
  182.6 52.1 %copy-start.21 = (bf16[128,462]{0,1:T(8,128)(2,1)}, bf16[128,462]{0,1:T(8,128)(2,1)S(1)}, u32[]{:S(2)}) copy-start(bf16[128,462]{0,1:T(8,128)(2,1)S(1)} %collective-permute-done.18) | copy-start | bytes 354820
  182.6 14.6 %collective-permute-start.20 = (bf16[128,462]{0,1:T(8,128)(2,1)S(1)}, bf16[128,462]{0,1:T(8,128)(2,1)S(1)}, u32[]{:S(2)}, u32[]{:S(2)}) collective-permute-start(bf16[128,462]{0,1:T(8,128)(2,1)S(1)} %collective-permute-done.18), channel_id=1, source_target_pairs={{0,480},{32,0},{64,32},{96,64},{128,96},{160,128},{192,160},{224,1... | collective-permute-start | bytes 354824 | tf_op jit(solution)/shard_map/ppermute | solution.py:51
  188.2 49.5 %copy-start.17 = (bf16[128,462]{0,1:T(8,128)(2,1)}, bf16[128,462]{0,1:T(8,128)(2,1)S(1)}, u32[]{:S(2)}) copy-start(bf16[128,462]{0,1:T(8,128)(2,1)S(1)} %collective-permute-done.19) | copy-start | bytes 354820
  188.2 14.2 %collective-permute-start.21 = (bf16[128,462]{0,1:T(8,128)(2,1)S(1)}, bf16[128,462]{0,1:T(8,128)(2,1)S(1)}, u32[]{:S(2)}, u32[]{:S(2)}) collective-permute-start(bf16[128,462]{0,1:T(8,128)(2,1)S(1)} %collective-permute-done.19), channel_id=1, source_target_pairs={{0,32},{32,64},{64,96},{96,128},{128,160},{160,192},{192,224},{224... | collective-permute-start | bytes 354824 | tf_op jit(solution)/shard_map/ppermute | solution.py:48
  190.2 22.1 %collective-permute-start.41 = (bf16[128,2,462]{0,2,1:T(8,128)(2,1)S(1)}, bf16[128,2,462]{0,2,1:T(8,128)(2,1)S(1)}, u32[]{:S(2)}, u32[]{:S(2)}) collective-permute-start(bf16[128,2,462]{0,2,1:T(8,128)(2,1)S(1)} %collective-permute-done.39), channel_id=1, source_target_pairs={{0,480},{32,0},{64,32},{96,64},{128,96},{160,128},{192,160},{224,1... | collective-permute-start | bytes 709640 | tf_op jit(solution)/shard_map/ppermute | solution.py:51
  195.3 22.1 %collective-permute-start.42 = (bf16[128,2,462]{0,2,1:T(8,128)(2,1)S(1)}, bf16[128,2,462]{0,2,1:T(8,128)(2,1)S(1)}, u32[]{:S(2)}, u32[]{:S(2)}) collective-permute-start(bf16[128,2,462]{0,2,1:T(8,128)(2,1)S(1)} %collective-permute-done.40), channel_id=1, source_target_pairs={{0,32},{32,64},{64,96},{96,128},{128,160},{160,192},{192,224},{224... | collective-permute-start | bytes 709640 | tf_op jit(solution)/shard_map/ppermute | solution.py:48
  197.2 37.5 %copy-start.23 = (bf16[128,462]{0,1:T(8,128)(2,1)}, bf16[128,462]{0,1:T(8,128)(2,1)S(1)}, u32[]{:S(2)}) copy-start(bf16[128,462]{0,1:T(8,128)(2,1)S(1)} %collective-permute-done.20) | copy-start | bytes 354820
  197.3 7.5 %collective-permute-start.22 = (bf16[128,462]{0,1:T(8,128)(2,1)S(1)}, bf16[128,462]{0,1:T(8,128)(2,1)S(1)}, u32[]{:S(2)}, u32[]{:S(2)}) collective-permute-start(bf16[128,462]{0,1:T(8,128)(2,1)S(1)} %collective-permute-done.20), channel_id=1, source_target_pairs={{0,480},{32,0},{64,32},{96,64},{128,96},{160,128},{192,160},{224,1... | collective-permute-start | bytes 354824 | tf_op jit(solution)/shard_map/ppermute | solution.py:51
  202.4 32.3 %copy-start.19 = (bf16[128,462]{0,1:T(8,128)(2,1)}, bf16[128,462]{0,1:T(8,128)(2,1)S(1)}, u32[]{:S(2)}) copy-start(bf16[128,462]{0,1:T(8,128)(2,1)S(1)} %collective-permute-done.21) | copy-start | bytes 354820
  202.4 7.9 %collective-permute-start.23 = (bf16[128,462]{0,1:T(8,128)(2,1)S(1)}, bf16[128,462]{0,1:T(8,128)(2,1)S(1)}, u32[]{:S(2)}, u32[]{:S(2)}) collective-permute-start(bf16[128,462]{0,1:T(8,128)(2,1)S(1)} %collective-permute-done.21), channel_id=1, source_target_pairs={{0,32},{32,64},{64,96},{96,128},{128,160},{160,192},{192,224},{224... | collective-permute-start | bytes 354824 | tf_op jit(solution)/shard_map/ppermute | solution.py:48
  204.8 14.6 %collective-permute-start.24 = (bf16[128,462]{0,1:T(8,128)(2,1)S(1)}, bf16[128,462]{0,1:T(8,128)(2,1)S(1)}, u32[]{:S(2)}, u32[]{:S(2)}) collective-permute-start(bf16[128,462]{0,1:T(8,128)(2,1)S(1)} %collective-permute-done.22), channel_id=1, source_target_pairs={{0,480},{32,0},{64,32},{96,64},{128,96},{160,128},{192,160},{224,1... | collective-permute-start | bytes 354824 | tf_op jit(solution)/shard_map/ppermute | solution.py:51
  210.4 14.2 %collective-permute-start.25 = (bf16[128,462]{0,1:T(8,128)(2,1)S(1)}, bf16[128,462]{0,1:T(8,128)(2,1)S(1)}, u32[]{:S(2)}, u32[]{:S(2)}) collective-permute-start(bf16[128,462]{0,1:T(8,128)(2,1)S(1)} %collective-permute-done.23), channel_id=1, source_target_pairs={{0,32},{32,64},{64,96},{96,128},{128,160},{160,192},{192,224},{224... | collective-permute-start | bytes 354824 | tf_op jit(solution)/shard_map/ppermute | solution.py:48
  212.3 220.2 %collective-permute-start.43 = (bf16[128,2,462]{0,2,1:T(8,128)(2,1)S(1)}, bf16[128,2,462]{0,2,1:T(8,128)(2,1)}, u32[]{:S(2)}, u32[]{:S(2)}) collective-permute-start(bf16[128,2,462]{0,2,1:T(8,128)(2,1)S(1)} %collective-permute-done.41), channel_id=1, source_target_pairs={{0,480},{32,0},{64,32},{96,64},{128,96},{160,128},{192,160},{224,1... | collective-permute-start | bytes 709640 | tf_op jit(solution)/shard_map/ppermute | solution.py:51
  217.4 245.0 %collective-permute-start.44 = (bf16[128,2,462]{0,2,1:T(8,128)(2,1)S(1)}, bf16[128,2,462]{0,2,1:T(8,128)(2,1)}, u32[]{:S(2)}, u32[]{:S(2)}) collective-permute-start(bf16[128,2,462]{0,2,1:T(8,128)(2,1)S(1)} %collective-permute-done.42), channel_id=1, source_target_pairs={{0,32},{32,64},{64,96},{96,128},{128,160},{160,192},{192,224},{224... | collective-permute-start | bytes 709640 | tf_op jit(solution)/shard_map/ppermute | solution.py:48
  219.4 7.5 %collective-permute-start.26 = (bf16[128,462]{0,1:T(8,128)(2,1)S(1)}, bf16[128,462]{0,1:T(8,128)(2,1)}, u32[]{:S(2)}, u32[]{:S(2)}) collective-permute-start(bf16[128,462]{0,1:T(8,128)(2,1)S(1)} %collective-permute-done.24), channel_id=1, source_target_pairs={{0,480},{32,0},{64,32},{96,64},{128,96},{160,128},{192,160},{224,1... | collective-permute-start | bytes 354824 | tf_op jit(solution)/shard_map/ppermute | solution.py:51
  224.5 8.0 %collective-permute-start.27 = (bf16[128,462]{0,1:T(8,128)(2,1)S(1)}, bf16[128,462]{0,1:T(8,128)(2,1)}, u32[]{:S(2)}, u32[]{:S(2)}) collective-permute-start(bf16[128,462]{0,1:T(8,128)(2,1)S(1)} %collective-permute-done.25), channel_id=1, source_target_pairs={{0,32},{32,64},{64,96},{96,128},{128,160},{160,192},{192,224},{224... | collective-permute-start | bytes 354824 | tf_op jit(solution)/shard_map/ppermute | solution.py:48
  226.9 341.0 %collective-permute-start.28 = (bf16[128,462]{0,1:T(8,128)(2,1)}, bf16[128,462]{0,1:T(8,128)(2,1)}, u32[]{:S(2)}, u32[]{:S(2)}) collective-permute-start(bf16[128,462]{0,1:T(8,128)(2,1)} %collective-permute-done.26), channel_id=1, source_target_pairs={{0,480},{32,0},{64,32},{96,64},{128,96},{160,128},{192,160},{224,1... | collective-permute-start | bytes 354824 | tf_op jit(solution)/shard_map/ppermute | solution.py:51
  232.6 348.7 %collective-permute-start.29 = (bf16[128,462]{0,1:T(8,128)(2,1)}, bf16[128,462]{0,1:T(8,128)(2,1)}, u32[]{:S(2)}, u32[]{:S(2)}) collective-permute-start(bf16[128,462]{0,1:T(8,128)(2,1)} %collective-permute-done.27), channel_id=1, source_target_pairs={{0,32},{32,64},{64,96},{96,128},{128,160},{160,192},{192,224},{224... | collective-permute-start | bytes 354824 | tf_op jit(solution)/shard_map/ppermute | solution.py:48
  282.4 32.6 %copy-start.10 = (bf16[128,2,462]{0,2,1:T(8,128)(2,1)S(1)}, bf16[128,2,462]{0,2,1:T(8,128)(2,1)}, u32[]{:S(2)}) copy-start(bf16[128,2,462]{0,2,1:T(8,128)(2,1)} %copy-done.9) | copy-start | bytes 709636
  299.4 44.6 %copy-start.8 = (bf16[128,2,462]{0,2,1:T(8,128)(2,1)S(1)}, bf16[128,2,462]{0,2,1:T(8,128)(2,1)}, u32[]{:S(2)}) copy-start(bf16[128,2,462]{0,2,1:T(8,128)(2,1)} %copy-done.7) | copy-start | bytes 709636
  483.0 31.8 %copy-start.24 = (bf16[128,462]{0,1:T(8,128)(2,1)S(1)}, bf16[128,462]{0,1:T(8,128)(2,1)}, u32[]{:S(2)}) copy-start(bf16[128,462]{0,1:T(8,128)(2,1)} %copy-done.23) | copy-start | bytes 354820
  489.6 37.8 %copy-start.20 = (bf16[128,462]{0,1:T(8,128)(2,1)S(1)}, bf16[128,462]{0,1:T(8,128)(2,1)}, u32[]{:S(2)}) copy-start(bf16[128,462]{0,1:T(8,128)(2,1)} %copy-done.19) | copy-start | bytes 354820
  502.3 38.2 %copy-start.26 = (bf16[128,462]{0,1:T(8,128)(2,1)S(1)}, bf16[128,462]{0,1:T(8,128)(2,1)}, u32[]{:S(2)}) copy-start(bf16[128,462]{0,1:T(8,128)(2,1)} %copy-done.25) | copy-start | bytes 354820
  508.5 32.2 %copy-start.32 = (bf16[128,462]{0,1:T(8,128)(2,1)S(1)}, bf16[128,462]{0,1:T(8,128)(2,1)}, u32[]{:S(2)}) copy-start(bf16[128,462]{0,1:T(8,128)(2,1)} %copy-done.31) | copy-start | bytes 354820
  515.0 38.2 %copy-start.28 = (bf16[128,462]{0,1:T(8,128)(2,1)S(1)}, bf16[128,462]{0,1:T(8,128)(2,1)}, u32[]{:S(2)}) copy-start(bf16[128,462]{0,1:T(8,128)(2,1)} %copy-done.27) | copy-start | bytes 354820
  (18 other events, 273.6 us)
Sparse Core Ops, SparseCore 0:
  11.1 63.0 all-gather.2
  86.3 57.4 all-gather.4
  597.6 103.6 reduce-scatter.1
where the time goes:
time: 721 us; the launch traced here: 708 us
  local copies, waits for them, and re-layouts  361 us (50%)
  starting transfers between devices  164 us (23%)
  waiting for transfers between devices  142 us (20%)
  matrix products  17.2 us (2%)
  between operations  15.8 us (2%)
  other arithmetic  7.71 us (1%)
    dynamic_update_slice x16, local copies, waits for them, and re-layouts, ring_all_gather(): out = lax.dynamic_update_index_in_dim(out, a, (me - s + n) % n, 0)  164 us
    dynamic_update_slice x14, local copies, waits for them, and re-layouts, ring_all_gather(): out = lax.dynamic_update_index_in_dim(out, b, (me + s) % n, 0)  143 us
    reduce_scatter x1, waiting for transfers between devices, shards(): lax.psum_scatter((contract_cols(gate_grad, w_gate) + contract_cols(up_gra...  93.5 us
    ppermute x14, starting transfers between devices, ring_all_gather(): b = lax.ppermute(b, axis, down)  76.6 us
    ppermute x7, starting transfers between devices, ring_reduce_scatter(): b = lax.ppermute(b.astype(wire_dtype), axis, down).astype(jnp.float32)  37.6 us
    all_gather x1, waiting for transfers between devices, shards(): all_grad_out = lax.all_gather(grad_out, 'col', axis=0, tiled=True)  36 us
    ppermute x16, starting transfers between devices, ring_all_gather(): a = lax.ppermute(a, axis, up)  32.8 us
    dynamic_update_slice x2, local copies, waits for them, and re-layouts, ring_all_gather(): out = lax.dynamic_update_index_in_dim(out, x, me, 0)  20.6 us
  transfers between devices with their start and end apart: 48, of which 13 were waited for; matrix products, arithmetic and copies ran while one was open for 54% of the time, Pallas kernels for 0%

commit v1 on v0

--- a/solution.py
+++ b/solution.py
@@ -81,7 +81,9 @@
     tokens_row, hidden_units = gate_pre.shape
     pre = jnp.stack([gate_pre, up_pre], axis=1)
     all_pre = ring_all_gather(pre, "row", n_row).reshape((n_row * tokens_row, 2, hidden_units))
-    all_grad_out = lax.all_gather(grad_out, "col", axis=0, tiled=True)
+    all_grad_out = jnp.concatenate(
+        lax.all_to_all(jnp.stack([grad_out] * lax.axis_size("col")), "col", 0, 0), axis=0
+    )
     all_inputs = lax.all_gather(inputs, "col", axis=0, tiled=True)
     part = contract_cols(all_grad_out, w_down).astype(jnp.bfloat16)
     part = part.reshape((n_row, tokens_row, hidden_units))

time: 721 us -> 695 us (0.964)
  waiting for transfers between devices: 142 us -> 103 us
  starting transfers between devices: 164 us -> 175 us
    all_gather x1 -> x0, waiting for transfers between devices: 36 us -> none  [shards(): all_grad_out = lax.all_gather(grad_out, 'col', axis=0, tiled=True)]
    all_to_all x0 -> x1, starting transfers between devices: none -> 9.68 us  [shards(): lax.all_to_all(jnp.stack([grad_out] * lax.axis_size('col')), 'col', 0, 0)]
  transfers between devices with their start and end apart: 48 -> 48, of which waited for: 13 -> 14; matrix products, arithmetic and copies ran while one was open for 54% -> 56% of each run, Pallas kernels for 0% -> 0%
where the time goes in v1:
time: 695 us; the launch traced here: 682 us
  local copies, waits for them, and re-layouts  364 us (52%)
  starting transfers between devices  175 us (25%)
  waiting for transfers between devices  103 us (15%)
  matrix products  16.9 us (2%)
  between operations  16.2 us (2%)
    dynamic_update_slice x16, local copies, waits for them, and re-layouts, ring_all_gather(): out = lax.dynamic_update_index_in_dim(out, a, (me - s + n) % n, 0)  164 us
    dynamic_update_slice x14, local copies, waits for them, and re-layouts, ring_all_gather(): out = lax.dynamic_update_index_in_dim(out, b, (me + s) % n, 0)  143 us
    reduce_scatter x1, waiting for transfers between devices, shards(): lax.psum_scatter((contract_cols(gate_grad, w_gate) + contract_cols(up_gra...  88 us
    ppermute x14, starting transfers between devices, ring_all_gather(): b = lax.ppermute(b, axis, down)  81.8 us
    ppermute x7, starting transfers between devices, ring_reduce_scatter(): b = lax.ppermute(b.astype(wire_dtype), axis, down).astype(jnp.float32)  37.6 us
    ppermute x16, starting transfers between devices, ring_all_gather(): a = lax.ppermute(a, axis, up)  30.7 us
    dynamic_update_slice x2, local copies, waits for them, and re-layouts, ring_all_gather(): out = lax.dynamic_update_index_in_dim(out, x, me, 0)  20.6 us
    ppermute x8, starting transfers between devices, ring_reduce_scatter(): a = lax.ppermute(a.astype(wire_dtype), axis, up).astype(jnp.float32)  15.5 us
  transfers between devices with their start and end apart: 48, of which 14 were waited for; matrix products, arithmetic and copies ran while one was open for 56% of the time, Pallas kernels for 0%

profile of v1, /device:TPU:2, one launch (start us, length us, event | category | flops | bytes accessed | tf_op | source)
XLA Modules:
  0.0 681.6 jit_solution(9949438827543421143)
XLA Ops:
  9.6 9.7 %all-to-all-start = ((bf16[32,64,512]{2,1,0:T(8,128)(2,1)}), bf16[32,64,512]{2,1,0:T(8,128)(2,1)S(1)}, u32[]{:S(2)}, u32[]{:S(2)}) async-start(bf16[32,64,512]{2,1,0:T(8,128)(2,1)} %stack.8), calls=%async_computation | async-start | bytes 4194304 | tf_op jit(solution)/shard_map/all_to_all | solution.py:85
  21.3 9.5 %collective-permute-start.31 = (bf16[128,2,462]{0,2,1:T(8,128)(2,1)S(1)}, bf16[128,2,462]{0,2,1:T(8,128)(2,1)}, u32[]{:S(2)}, u32[]{:S(2)}) collective-permute-start(bf16[128,2,462]{0,2,1:T(8,128)(2,1)S(1)} %get-tuple-element.22), channel_id=1, source_target_pairs={{0,480},{32,0},{64,32},{96,64},{128,96},{160,128},{192,160},{224,1... | collective-permute-start | bytes 709640 | tf_op jit(solution)/shard_map/ppermute | solution.py:51
  30.8 4.1 collective-permute-done.30
  37.1 5.1 collective-permute-start.33
  42.2 3.1 collective-permute-done.32
  47.3 2.5 convolution_convert_fusion
  50.8 4.8 constant_dynamic-slice_fusion.15
  57.7 9.4 %collective-permute-start.35 = (bf16[128,2,462]{0,2,1:T(8,128)(2,1)}, bf16[128,2,462]{0,2,1:T(8,128)(2,1)S(1)}, u32[]{:S(2)}, u32[]{:S(2)}) collective-permute-start(bf16[128,2,462]{0,2,1:T(8,128)(2,1)} %collective-permute-done.33), channel_id=1, source_target_pairs={{0,480},{32,0},{64,32},{96,64},{128,96},{160,128},{192,160},{224,1... | collective-permute-start | bytes 709640 | tf_op jit(solution)/shard_map/ppermute | solution.py:51
  69.0 5.1 collective-permute-start.8
  78.1 5.1 collective-permute-start.9
  87.2 5.1 collective-permute-start.10
  94.8 5.5 collective-permute-start.11
  102.7 5.5 collective-permute-start.12
  110.7 5.5 collective-permute-start.13
  119.2 5.6 collective-permute-start.14
  127.2 5.1 collective-permute-start.37
  136.4 5.1 collective-permute-start.16
  141.5 2.5 collective-permute-done.15
  146.0 5.1 collective-permute-start.39
  153.1 5.1 collective-permute-start.18
  160.6 5.5 collective-permute-start.20
  168.2 5.1 collective-permute-start.41
  175.3 5.1 collective-permute-start.22
  183.3 5.6 collective-permute-start.24
  191.2 5.1 collective-permute-start.43
  198.3 5.1 collective-permute-start.26
  205.8 5.6 collective-permute-start.28
  216.5 14.4 %dynamic_update_slice.114 = bf16[16,128,2,462]{1,0,3,2:T(8,128)(2,1)} dynamic-update-slice(bf16[16,128,2,462]{1,0,3,2:T(8,128)(2,1)} %broadcast_in_dim.121, bf16[1,128,2,462]{1,0,3,2:T(2,128)(2,1)S(1)} %copy.56, s32[]{:T(128)S(6)} %select_n.304, s32[]{:T(128)} %constant.338.clone.1, s32[]{:T(128)} %constant.338.clone.1, s32[]{:T(128)} %constant.338.clone.1) | dynamic-update-slice | bytes 473092 | tf_op jit(solution)/shard_map/jit(dynamic_update_index_in_dim)/dynamic_update_slice | solution.py:44
  232.7 14.3 %dynamic_update_slice.115 = bf16[16,128,2,462]{1,0,3,2:T(8,128)(2,1)} dynamic-update-slice(bf16[16,128,2,462]{1,0,3,2:T(8,128)(2,1)} %dynamic_update_slice.114, bf16[1,128,2,462]{1,0,3,2:T(2,128)(2,1)S(1)} %copy.57, s32[]{:T(128)S(6)} %select_n.306, s32[]{:T(128)} %constant.338.clone.1, s32[]{:T(128)} %constant.338.clone.1, s32[]{:T(128)} %constant.338.clone.1) | dynamic-update-slice | bytes 473092 | tf_op jit(solution)/shard_map/jit(dynamic_update_index_in_dim)/dynamic_update_slice | solution.py:49
  246.9 14.3 %dynamic_update_slice.116 = bf16[16,128,2,462]{1,0,3,2:T(8,128)(2,1)} dynamic-update-slice(bf16[16,128,2,462]{1,0,3,2:T(8,128)(2,1)} %dynamic_update_slice.115, bf16[1,128,2,462]{1,0,3,2:T(2,128)(2,1)S(1)} %copy.58, s32[]{:T(128)S(6)} %select_n.308, s32[]{:T(128)} %constant.338.clone.1, s32[]{:T(128)} %constant.338.clone.1, s32[]{:T(128)} %constant.338.clone.1) | dynamic-update-slice | bytes 473092 | tf_op jit(solution)/shard_map/jit(dynamic_update_index_in_dim)/dynamic_update_slice | solution.py:52
  263.9 14.3 %dynamic_update_slice.117 = bf16[16,128,2,462]{1,0,3,2:T(8,128)(2,1)} dynamic-update-slice(bf16[16,128,2,462]{1,0,3,2:T(8,128)(2,1)} %dynamic_update_slice.116, bf16[1,128,2,462]{1,0,3,2:T(2,128)(2,1)S(1)} %copy.59, s32[]{:T(128)S(6)} %select_n.310, s32[]{:T(128)} %constant.338.clone.1, s32[]{:T(128)} %constant.338.clone.1, s32[]{:T(128)} %constant.338.clone.1) | dynamic-update-slice | bytes 473092 | tf_op jit(solution)/shard_map/jit(dynamic_update_index_in_dim)/dynamic_update_slice | solution.py:49
  278.2 14.3 %dynamic_update_slice.118 = bf16[16,128,2,462]{1,0,3,2:T(8,128)(2,1)} dynamic-update-slice(bf16[16,128,2,462]{1,0,3,2:T(8,128)(2,1)} %dynamic_update_slice.117, bf16[1,128,2,462]{1,0,3,2:T(2,128)(2,1)S(1)} %copy.60, s32[]{:T(128)S(6)} %select_n.312, s32[]{:T(128)} %constant.338.clone.1, s32[]{:T(128)} %constant.338.clone.1, s32[]{:T(128)} %constant.338.clone.1) | dynamic-update-slice | bytes 473092 | tf_op jit(solution)/shard_map/jit(dynamic_update_index_in_dim)/dynamic_update_slice | solution.py:52
  294.2 14.3 %dynamic_update_slice.119 = bf16[16,128,2,462]{1,0,3,2:T(8,128)(2,1)} dynamic-update-slice(bf16[16,128,2,462]{1,0,3,2:T(8,128)(2,1)} %dynamic_update_slice.118, bf16[1,128,2,462]{1,0,3,2:T(2,128)(2,1)S(1)} %copy.61, s32[]{:T(128)S(6)} %select_n.314, s32[]{:T(128)} %constant.338.clone.1, s32[]{:T(128)} %constant.338.clone.1, s32[]{:T(128)} %constant.338.clone.1) | dynamic-update-slice | bytes 473092 | tf_op jit(solution)/shard_map/jit(dynamic_update_index_in_dim)/dynamic_update_slice | solution.py:49
  308.5 14.3 %dynamic_update_slice.120 = bf16[16,128,2,462]{1,0,3,2:T(8,128)(2,1)} dynamic-update-slice(bf16[16,128,2,462]{1,0,3,2:T(8,128)(2,1)} %dynamic_update_slice.119, bf16[1,128,2,462]{1,0,3,2:T(2,128)(2,1)S(1)} %copy.62, s32[]{:T(128)S(6)} %select_n.316, s32[]{:T(128)} %constant.338.clone.1, s32[]{:T(128)} %constant.338.clone.1, s32[]{:T(128)} %constant.338.clone.1) | dynamic-update-slice | bytes 473092 | tf_op jit(solution)/shard_map/jit(dynamic_update_index_in_dim)/dynamic_update_slice | solution.py:52
  323.5 14.3 %dynamic_update_slice.121 = bf16[16,128,2,462]{1,0,3,2:T(8,128)(2,1)} dynamic-update-slice(bf16[16,128,2,462]{1,0,3,2:T(8,128)(2,1)} %dynamic_update_slice.120, bf16[1,128,2,462]{1,0,3,2:T(2,128)(2,1)S(1)} %copy.63, s32[]{:T(128)S(6)} %select_n.318, s32[]{:T(128)} %constant.338.clone.1, s32[]{:T(128)} %constant.338.clone.1, s32[]{:T(128)} %constant.338.clone.1) | dynamic-update-slice | bytes 473092 | tf_op jit(solution)/shard_map/jit(dynamic_update_index_in_dim)/dynamic_update_slice | solution.py:49
  337.8 14.3 %dynamic_update_slice.122 = bf16[16,128,2,462]{1,0,3,2:T(8,128)(2,1)} dynamic-update-slice(bf16[16,128,2,462]{1,0,3,2:T(8,128)(2,1)} %dynamic_update_slice.121, bf16[1,128,2,462]{1,0,3,2:T(2,128)(2,1)S(1)} %copy.64, s32[]{:T(128)S(6)} %select_n.320, s32[]{:T(128)} %constant.338.clone.1, s32[]{:T(128)} %constant.338.clone.1, s32[]{:T(128)} %constant.338.clone.1) | dynamic-update-slice | bytes 473092 | tf_op jit(solution)/shard_map/jit(dynamic_update_index_in_dim)/dynamic_update_slice | solution.py:52
  352.9 14.3 %dynamic_update_slice.123 = bf16[16,128,2,462]{1,0,3,2:T(8,128)(2,1)} dynamic-update-slice(bf16[16,128,2,462]{1,0,3,2:T(8,128)(2,1)} %dynamic_update_slice.122, bf16[1,128,2,462]{1,0,3,2:T(2,128)(2,1)S(1)} %copy.65, s32[]{:T(128)S(6)} %select_n.322, s32[]{:T(128)} %constant.338.clone.1, s32[]{:T(128)} %constant.338.clone.1, s32[]{:T(128)} %constant.338.clone.1) | dynamic-update-slice | bytes 473092 | tf_op jit(solution)/shard_map/jit(dynamic_update_index_in_dim)/dynamic_update_slice | solution.py:49
  367.2 14.3 %dynamic_update_slice.124 = bf16[16,128,2,462]{1,0,3,2:T(8,128)(2,1)} dynamic-update-slice(bf16[16,128,2,462]{1,0,3,2:T(8,128)(2,1)} %dynamic_update_slice.123, bf16[1,128,2,462]{1,0,3,2:T(2,128)(2,1)S(1)} %copy.66, s32[]{:T(128)S(6)} %select_n.324, s32[]{:T(128)} %constant.338.clone.1, s32[]{:T(128)} %constant.338.clone.1, s32[]{:T(128)} %constant.338.clone.1) | dynamic-update-slice | bytes 473092 | tf_op jit(solution)/shard_map/jit(dynamic_update_index_in_dim)/dynamic_update_slice | solution.py:52
  382.2 14.5 %dynamic_update_slice.125 = bf16[16,128,2,462]{1,0,3,2:T(8,128)(2,1)} dynamic-update-slice(bf16[16,128,2,462]{1,0,3,2:T(8,128)(2,1)} %dynamic_update_slice.124, bf16[1,128,2,462]{1,0,3,2:T(2,128)(2,1)S(1)} %copy.67, s32[]{:T(128)S(6)} %select_n.326, s32[]{:T(128)} %constant.338.clone.1, s32[]{:T(128)} %constant.338.clone.1, s32[]{:T(128)} %constant.338.clone.1) | dynamic-update-slice | bytes 473092 | tf_op jit(solution)/shard_map/jit(dynamic_update_index_in_dim)/dynamic_update_slice | solution.py:49
  396.7 14.3 %dynamic_update_slice.126 = bf16[16,128,2,462]{1,0,3,2:T(8,128)(2,1)} dynamic-update-slice(bf16[16,128,2,462]{1,0,3,2:T(8,128)(2,1)} %dynamic_update_slice.125, bf16[1,128,2,462]{1,0,3,2:T(2,128)(2,1)S(1)} %copy.68, s32[]{:T(128)S(6)} %select_n.328, s32[]{:T(128)} %constant.338.clone.1, s32[]{:T(128)} %constant.338.clone.1, s32[]{:T(128)} %constant.338.clone.1) | dynamic-update-slice | bytes 473092 | tf_op jit(solution)/shard_map/jit(dynamic_update_index_in_dim)/dynamic_update_slice | solution.py:52
  412.7 14.3 %dynamic_update_slice.127 = bf16[16,128,2,462]{1,0,3,2:T(8,128)(2,1)} dynamic-update-slice(bf16[16,128,2,462]{1,0,3,2:T(8,128)(2,1)} %dynamic_update_slice.126, bf16[1,128,2,462]{1,0,3,2:T(2,128)(2,1)S(1)} %copy.69, s32[]{:T(128)S(6)} %select_n.330, s32[]{:T(128)} %constant.338.clone.1, s32[]{:T(128)} %constant.338.clone.1, s32[]{:T(128)} %constant.338.clone.1) | dynamic-update-slice | bytes 473092 | tf_op jit(solution)/shard_map/jit(dynamic_update_index_in_dim)/dynamic_update_slice | solution.py:49
  427.0 14.3 %dynamic_update_slice.128 = bf16[16,128,2,462]{1,0,3,2:T(8,128)(2,1)} dynamic-update-slice(bf16[16,128,2,462]{1,0,3,2:T(8,128)(2,1)} %dynamic_update_slice.127, bf16[1,128,2,462]{1,0,3,2:T(2,128)(2,1)S(1)} %copy.70, s32[]{:T(128)S(6)} %select_n.332, s32[]{:T(128)} %constant.338.clone.1, s32[]{:T(128)} %constant.338.clone.1, s32[]{:T(128)} %constant.338.clone.1) | dynamic-update-slice | bytes 473092 | tf_op jit(solution)/shard_map/jit(dynamic_update_index_in_dim)/dynamic_update_slice | solution.py:52
  442.5 14.3 %dynamic_update_slice.129 = bf16[16,128,2,462]{1,0,3,2:T(8,128)(2,1)} dynamic-update-slice(bf16[16,128,2,462]{1,0,3,2:T(8,128)(2,1)} %dynamic_update_slice.128, bf16[1,128,2,462]{1,0,3,2:T(2,128)(2,1)S(1)} %copy.71, s32[]{:T(128)S(6)} %select_n.334, s32[]{:T(128)} %constant.338.clone.1, s32[]{:T(128)} %constant.338.clone.1, s32[]{:T(128)} %constant.338.clone.1) | dynamic-update-slice | bytes 473092 | tf_op jit(solution)/shard_map/jit(dynamic_update_index_in_dim)/dynamic_update_slice | solution.py:49
  456.8 4.5 reshape.57
  461.8 6.2 dynamic_update_slice.98
  468.4 6.2 dynamic_update_slice.99
  474.6 6.2 dynamic_update_slice.100
  481.1 6.2 dynamic_update_slice.101
  487.3 6.2 dynamic_update_slice.102
  493.9 6.2 dynamic_update_slice.103
  500.0 6.2 dynamic_update_slice.104
  506.6 6.6 dynamic_update_slice.105
  513.1 6.2 dynamic_update_slice.106
  519.7 6.2 dynamic_update_slice.107
  525.9 6.2 dynamic_update_slice.108
  533.3 6.2 dynamic_update_slice.109
  539.5 6.2 dynamic_update_slice.110
  547.8 6.2 dynamic_update_slice.111
  554.0 6.2 dynamic_update_slice.112
  561.2 6.2 dynamic_update_slice.113
  573.6 2.7 add_convert_fusion
  576.3 4.7 fusion.22
  581.1 3.7 fusion.25
  586.7 88.0 %reduce-scatter.2.cloned.1.call-done = bf16[64,512]{1,0:T(8,128)(2,1)} async-done(((bf16[2048,512]{1,0:T(8,128)(2,1)}), bf16[64,512]{1,0:T(8,128)(2,1)}) %reduce-scatter.2.cloned.1.call-update) | async-done | bytes 65552 | tf_op jit(solution)/shard_map/reduce_scatter | solution.py:98
  (208 shorter events, 87.9 us)
Async XLA Ops:
  7.2 565.0 %copy-start = (bf16[512,462]{0,1:T(8,128)(2,1)S(1)}, bf16[512,462]{0,1:T(8,128)(2,1)}, u32[]{:S(2)}) copy-start(bf16[512,462]{0,1:T(8,128)(2,1)} %param.10) | copy-start | bytes 1419268
  9.6 37.7 %all-to-all-start = ((bf16[32,64,512]{2,1,0:T(8,128)(2,1)}), bf16[32,64,512]{2,1,0:T(8,128)(2,1)S(1)}, u32[]{:S(2)}, u32[]{:S(2)}) async-start(bf16[32,64,512]{2,1,0:T(8,128)(2,1)} %stack.8), calls=%async_computation | async-start | bytes 4194304 | tf_op jit(solution)/shard_map/all_to_all | solution.py:85
  19.3 561.8 %all-gather.2.cloned.1.call-start = ((), (), s32[]{:S(2)}) async-start(), calls=%async_computation.3 | async-start | bytes 2162688 | tf_op jit(solution)/shard_map/all_gather | solution.py:87
  19.4 15.5 %collective-permute-start.30 = (bf16[128,2,462]{0,2,1:T(8,128)(2,1)S(1)}, bf16[128,2,462]{0,2,1:T(8,128)(2,1)S(1)}, u32[]{:S(2)}, u32[]{:S(2)}) collective-permute-start(bf16[128,2,462]{0,2,1:T(8,128)(2,1)S(1)} %get-tuple-element.22), channel_id=1, source_target_pairs={{0,32},{32,64},{64,96},{96,128},{128,160},{160,192},{192,224},{224... | collective-permute-start | bytes 709640 | tf_op jit(solution)/shard_map/ppermute | solution.py:48
  21.3 15.7 %collective-permute-start.31 = (bf16[128,2,462]{0,2,1:T(8,128)(2,1)S(1)}, bf16[128,2,462]{0,2,1:T(8,128)(2,1)}, u32[]{:S(2)}, u32[]{:S(2)}) collective-permute-start(bf16[128,2,462]{0,2,1:T(8,128)(2,1)S(1)} %get-tuple-element.22), channel_id=1, source_target_pairs={{0,480},{32,0},{64,32},{96,64},{128,96},{160,128},{192,160},{224,1... | collective-permute-start | bytes 709640 | tf_op jit(solution)/shard_map/ppermute | solution.py:51
  34.9 10.4 %collective-permute-start.32 = (bf16[128,2,462]{0,2,1:T(8,128)(2,1)S(1)}, bf16[128,2,462]{0,2,1:T(8,128)(2,1)}, u32[]{:S(2)}, u32[]{:S(2)}) collective-permute-start(bf16[128,2,462]{0,2,1:T(8,128)(2,1)S(1)} %collective-permute-done.30), channel_id=1, source_target_pairs={{0,32},{32,64},{64,96},{96,128},{128,160},{160,192},{192,224},{224... | collective-permute-start | bytes 709640 | tf_op jit(solution)/shard_map/ppermute | solution.py:48
  37.1 20.6 %collective-permute-start.33 = (bf16[128,2,462]{0,2,1:T(8,128)(2,1)}, bf16[128,2,462]{0,2,1:T(8,128)(2,1)}, u32[]{:S(2)}, u32[]{:S(2)}) collective-permute-start(bf16[128,2,462]{0,2,1:T(8,128)(2,1)} %collective-permute-done.31), channel_id=1, source_target_pairs={{0,480},{32,0},{64,32},{96,64},{128,96},{160,128},{192,160},{224,1... | collective-permute-start | bytes 709640 | tf_op jit(solution)/shard_map/ppermute | solution.py:51
  45.4 21.7 %collective-permute-start.34 = (bf16[128,2,462]{0,2,1:T(8,128)(2,1)}, bf16[128,2,462]{0,2,1:T(8,128)(2,1)}, u32[]{:S(2)}, u32[]{:S(2)}) collective-permute-start(bf16[128,2,462]{0,2,1:T(8,128)(2,1)} %collective-permute-done.32), channel_id=1, source_target_pairs={{0,32},{32,64},{64,96},{96,128},{128,160},{160,192},{192,224},{224... | collective-permute-start | bytes 709640 | tf_op jit(solution)/shard_map/ppermute | solution.py:48
  55.5 36.8 %copy-start.5 = (bf16[1,128,462]{1,0,2:T(2,128)(2,1)S(1)}, bf16[1,128,462]{1,0,2:T(2,128)(2,1)}, u32[]{:S(2)}) copy-start(bf16[1,128,462]{1,0,2:T(2,128)(2,1)} %get-tuple-element.17) | copy-start | bytes 354820
  55.6 18.6 %collective-permute-start = (bf16[128,462]{0,1:T(8,128)(2,1)S(1)}, bf16[128,462]{0,1:T(8,128)(2,1)}, u32[]{:S(2)}, u32[]{:S(2)}) collective-permute-start(bf16[128,462]{0,1:T(8,128)(2,1)S(1)} %bitcast.211), channel_id=1, source_target_pairs={{0,32},{32,64},{64,96},{96,128},{128,160},{160,192},{192,224},{224... | collective-permute-start | bytes 354824 | tf_op jit(solution)/shard_map/ppermute | solution.py:70
  57.6 617.0 %reduce-scatter.2.cloned.1.call-start = ((), (), s32[]{:S(2)}) async-start(), calls=%async_computation.2 | async-start | bytes 2162688 | tf_op jit(solution)/shard_map/reduce_scatter | solution.py:98
  57.7 69.4 %collective-permute-start.35 = (bf16[128,2,462]{0,2,1:T(8,128)(2,1)}, bf16[128,2,462]{0,2,1:T(8,128)(2,1)S(1)}, u32[]{:S(2)}, u32[]{:S(2)}) collective-permute-start(bf16[128,2,462]{0,2,1:T(8,128)(2,1)} %collective-permute-done.33), channel_id=1, source_target_pairs={{0,480},{32,0},{64,32},{96,64},{128,96},{160,128},{192,160},{224,1... | collective-permute-start | bytes 709640 | tf_op jit(solution)/shard_map/ppermute | solution.py:51
  67.1 65.2 %collective-permute-start.36 = (bf16[128,2,462]{0,2,1:T(8,128)(2,1)}, bf16[128,2,462]{0,2,1:T(8,128)(2,1)S(1)}, u32[]{:S(2)}, u32[]{:S(2)}) collective-permute-start(bf16[128,2,462]{0,2,1:T(8,128)(2,1)} %collective-permute-done.34), channel_id=1, source_target_pairs={{0,32},{32,64},{64,96},{96,128},{128,160},{160,192},{192,224},{224... | collective-permute-start | bytes 709640 | tf_op jit(solution)/shard_map/ppermute | solution.py:48
  69.0 8.1 %collective-permute-start.8 = (bf16[128,462]{0,1:T(8,128)(2,1)S(1)}, bf16[128,462]{0,1:T(8,128)(2,1)S(1)}, u32[]{:S(2)}, u32[]{:S(2)}) collective-permute-start(bf16[128,462]{0,1:T(8,128)(2,1)S(1)} %bitcast.212), channel_id=1, source_target_pairs={{0,480},{32,0},{64,32},{96,64},{128,96},{160,128},{192,160},{224,1... | collective-permute-start | bytes 354824 | tf_op jit(solution)/shard_map/ppermute | solution.py:74
  75.2 8.1 %collective-permute-start.1 = (bf16[128,462]{0,1:T(8,128)(2,1)S(1)}, bf16[128,462]{0,1:T(8,128)(2,1)S(1)}, u32[]{:S(2)}, u32[]{:S(2)}) collective-permute-start(bf16[128,462]{0,1:T(8,128)(2,1)S(1)} %fusion.39), channel_id=1, source_target_pairs={{0,32},{32,64},{64,96},{96,128},{128,160},{160,192},{192,224},{224... | collective-permute-start | bytes 354824 | tf_op jit(solution)/shard_map/ppermute | solution.py:70
  78.1 8.1 %collective-permute-start.9 = (bf16[128,462]{0,1:T(8,128)(2,1)S(1)}, bf16[128,462]{0,1:T(8,128)(2,1)S(1)}, u32[]{:S(2)}, u32[]{:S(2)}) collective-permute-start(bf16[128,462]{0,1:T(8,128)(2,1)S(1)} %fusion.32), channel_id=1, source_target_pairs={{0,480},{32,0},{64,32},{96,64},{128,96},{160,128},{192,160},{224,1... | collective-permute-start | bytes 354824 | tf_op jit(solution)/shard_map/ppermute | solution.py:74
  84.3 8.1 %collective-permute-start.2 = (bf16[128,462]{0,1:T(8,128)(2,1)S(1)}, bf16[128,462]{0,1:T(8,128)(2,1)S(1)}, u32[]{:S(2)}, u32[]{:S(2)}) collective-permute-start(bf16[128,462]{0,1:T(8,128)(2,1)S(1)} %fusion.38), channel_id=1, source_target_pairs={{0,32},{32,64},{64,96},{96,128},{128,160},{160,192},{192,224},{224... | collective-permute-start | bytes 354824 | tf_op jit(solution)/shard_map/ppermute | solution.py:70
  87.2 7.5 %collective-permute-start.10 = (bf16[128,462]{0,1:T(8,128)(2,1)S(1)}, bf16[128,462]{0,1:T(8,128)(2,1)S(1)}, u32[]{:S(2)}, u32[]{:S(2)}) collective-permute-start(bf16[128,462]{0,1:T(8,128)(2,1)S(1)} %fusion.31), channel_id=1, source_target_pairs={{0,480},{32,0},{64,32},{96,64},{128,96},{160,128},{192,160},{224,1... | collective-permute-start | bytes 354824 | tf_op jit(solution)/shard_map/ppermute | solution.py:74
  92.4 7.9 %collective-permute-start.3 = (bf16[128,462]{0,1:T(8,128)(2,1)S(1)}, bf16[128,462]{0,1:T(8,128)(2,1)S(1)}, u32[]{:S(2)}, u32[]{:S(2)}) collective-permute-start(bf16[128,462]{0,1:T(8,128)(2,1)S(1)} %fusion.37), channel_id=1, source_target_pairs={{0,32},{32,64},{64,96},{96,128},{128,160},{160,192},{192,224},{224... | collective-permute-start | bytes 354824 | tf_op jit(solution)/shard_map/ppermute | solution.py:70
  94.8 7.9 %collective-permute-start.11 = (bf16[128,462]{0,1:T(8,128)(2,1)S(1)}, bf16[128,462]{0,1:T(8,128)(2,1)S(1)}, u32[]{:S(2)}, u32[]{:S(2)}) collective-permute-start(bf16[128,462]{0,1:T(8,128)(2,1)S(1)} %fusion.30), channel_id=1, source_target_pairs={{0,480},{32,0},{64,32},{96,64},{128,96},{160,128},{192,160},{224,1... | collective-permute-start | bytes 354824 | tf_op jit(solution)/shard_map/ppermute | solution.py:74
  100.4 7.9 %collective-permute-start.4 = (bf16[128,462]{0,1:T(8,128)(2,1)S(1)}, bf16[128,462]{0,1:T(8,128)(2,1)S(1)}, u32[]{:S(2)}, u32[]{:S(2)}) collective-permute-start(bf16[128,462]{0,1:T(8,128)(2,1)S(1)} %fusion.36), channel_id=1, source_target_pairs={{0,32},{32,64},{64,96},{96,128},{128,160},{160,192},{192,224},{224... | collective-permute-start | bytes 354824 | tf_op jit(solution)/shard_map/ppermute | solution.py:70
  102.7 7.9 %collective-permute-start.12 = (bf16[128,462]{0,1:T(8,128)(2,1)S(1)}, bf16[128,462]{0,1:T(8,128)(2,1)S(1)}, u32[]{:S(2)}, u32[]{:S(2)}) collective-permute-start(bf16[128,462]{0,1:T(8,128)(2,1)S(1)} %fusion.29), channel_id=1, source_target_pairs={{0,480},{32,0},{64,32},{96,64},{128,96},{160,128},{192,160},{224,1... | collective-permute-start | bytes 354824 | tf_op jit(solution)/shard_map/ppermute | solution.py:74
  108.3 7.9 %collective-permute-start.5 = (bf16[128,462]{0,1:T(8,128)(2,1)S(1)}, bf16[128,462]{0,1:T(8,128)(2,1)S(1)}, u32[]{:S(2)}, u32[]{:S(2)}) collective-permute-start(bf16[128,462]{0,1:T(8,128)(2,1)S(1)} %fusion.35), channel_id=1, source_target_pairs={{0,32},{32,64},{64,96},{96,128},{128,160},{160,192},{192,224},{224... | collective-permute-start | bytes 354824 | tf_op jit(solution)/shard_map/ppermute | solution.py:70
  110.7 8.5 %collective-permute-start.13 = (bf16[128,462]{0,1:T(8,128)(2,1)S(1)}, bf16[128,462]{0,1:T(8,128)(2,1)S(1)}, u32[]{:S(2)}, u32[]{:S(2)}) collective-permute-start(bf16[128,462]{0,1:T(8,128)(2,1)S(1)} %fusion.28), channel_id=1, source_target_pairs={{0,480},{32,0},{64,32},{96,64},{128,96},{160,128},{192,160},{224,1... | collective-permute-start | bytes 354824 | tf_op jit(solution)/shard_map/ppermute | solution.py:74
  116.3 8.9 %collective-permute-start.6 = (bf16[128,462]{0,1:T(8,128)(2,1)S(1)}, bf16[128,462]{0,1:T(8,128)(2,1)S(1)}, u32[]{:S(2)}, u32[]{:S(2)}) collective-permute-start(bf16[128,462]{0,1:T(8,128)(2,1)S(1)} %fusion.34), channel_id=1, source_target_pairs={{0,32},{32,64},{64,96},{96,128},{128,160},{160,192},{192,224},{224... | collective-permute-start | bytes 354824 | tf_op jit(solution)/shard_map/ppermute | solution.py:70
  119.2 15.0 %collective-permute-start.14 = (bf16[128,462]{0,1:T(8,128)(2,1)S(1)}, bf16[128,462]{0,1:T(8,128)(2,1)S(1)}, u32[]{:S(2)}, u32[]{:S(2)}) collective-permute-start(bf16[128,462]{0,1:T(8,128)(2,1)S(1)} %fusion.27), channel_id=1, source_target_pairs={{0,480},{32,0},{64,32},{96,64},{128,96},{160,128},{192,160},{224,1... | collective-permute-start | bytes 354824 | tf_op jit(solution)/shard_map/ppermute | solution.py:74
  125.2 9.2 %collective-permute-start.7 = (bf16[128,462]{0,1:T(8,128)(2,1)S(1)}, bf16[128,462]{0,1:T(8,128)(2,1)S(1)}, u32[]{:S(2)}, u32[]{:S(2)}) collective-permute-start(bf16[128,462]{0,1:T(8,128)(2,1)S(1)} %fusion.33), channel_id=1, source_target_pairs={{0,32},{32,64},{64,96},{96,128},{128,160},{160,192},{192,224},{224... | collective-permute-start | bytes 354824 | tf_op jit(solution)/shard_map/ppermute | solution.py:70
  127.2 18.8 %collective-permute-start.37 = (bf16[128,2,462]{0,2,1:T(8,128)(2,1)S(1)}, bf16[128,2,462]{0,2,1:T(8,128)(2,1)S(1)}, u32[]{:S(2)}, u32[]{:S(2)}) collective-permute-start(bf16[128,2,462]{0,2,1:T(8,128)(2,1)S(1)} %collective-permute-done.35), channel_id=1, source_target_pairs={{0,480},{32,0},{64,32},{96,64},{128,96},{160,128},{192,160},{224,1... | collective-permute-start | bytes 709640 | tf_op jit(solution)/shard_map/ppermute | solution.py:51
  132.3 18.8 %collective-permute-start.38 = (bf16[128,2,462]{0,2,1:T(8,128)(2,1)S(1)}, bf16[128,2,462]{0,2,1:T(8,128)(2,1)S(1)}, u32[]{:S(2)}, u32[]{:S(2)}) collective-permute-start(bf16[128,2,462]{0,2,1:T(8,128)(2,1)S(1)} %collective-permute-done.36), channel_id=1, source_target_pairs={{0,32},{32,64},{64,96},{96,128},{128,160},{160,192},{192,224},{224... | collective-permute-start | bytes 709640 | tf_op jit(solution)/shard_map/ppermute | solution.py:48
  134.5 9.6 %collective-permute-start.15 = (bf16[128,462]{0,1:T(8,128)(2,1)S(1)}, bf16[128,462]{0,1:T(8,128)(2,1)S(1)}, u32[]{:S(2)}, u32[]{:S(2)}) collective-permute-start(bf16[128,462]{0,1:T(8,128)(2,1)S(1)} %fusion.41), channel_id=1, source_target_pairs={{0,32},{32,64},{64,96},{96,128},{128,160},{160,192},{192,224},{224... | collective-permute-start | bytes 354824 | tf_op jit(solution)/shard_map/ppermute | solution.py:48
  136.4 16.7 %collective-permute-start.16 = (bf16[128,462]{0,1:T(8,128)(2,1)S(1)}, bf16[128,462]{0,1:T(8,128)(2,1)S(1)}, u32[]{:S(2)}, u32[]{:S(2)}) collective-permute-start(bf16[128,462]{0,1:T(8,128)(2,1)S(1)} %fusion.41), channel_id=1, source_target_pairs={{0,480},{32,0},{64,32},{96,64},{128,96},{160,128},{192,160},{224,1... | collective-permute-start | bytes 354824 | tf_op jit(solution)/shard_map/ppermute | solution.py:51
  144.1 72.4 %copy-start.15 = (bf16[128,462]{0,1:T(8,128)(2,1)}, bf16[128,462]{0,1:T(8,128)(2,1)S(1)}, u32[]{:S(2)}) copy-start(bf16[128,462]{0,1:T(8,128)(2,1)S(1)} %collective-permute-done.15) | copy-start | bytes 354820
  144.1 14.2 %collective-permute-start.17 = (bf16[128,462]{0,1:T(8,128)(2,1)S(1)}, bf16[128,462]{0,1:T(8,128)(2,1)S(1)}, u32[]{:S(2)}, u32[]{:S(2)}) collective-permute-start(bf16[128,462]{0,1:T(8,128)(2,1)S(1)} %collective-permute-done.15), channel_id=1, source_target_pairs={{0,32},{32,64},{64,96},{96,128},{128,160},{160,192},{192,224},{224... | collective-permute-start | bytes 354824 | tf_op jit(solution)/shard_map/ppermute | solution.py:48
  146.0 22.1 %collective-permute-start.39 = (bf16[128,2,462]{0,2,1:T(8,128)(2,1)S(1)}, bf16[128,2,462]{0,2,1:T(8,128)(2,1)S(1)}, u32[]{:S(2)}, u32[]{:S(2)}) collective-permute-start(bf16[128,2,462]{0,2,1:T(8,128)(2,1)S(1)} %collective-permute-done.37), channel_id=1, source_target_pairs={{0,480},{32,0},{64,32},{96,64},{128,96},{160,128},{192,160},{224,1... | collective-permute-start | bytes 709640 | tf_op jit(solution)/shard_map/ppermute | solution.py:51
  151.2 22.1 %collective-permute-start.40 = (bf16[128,2,462]{0,2,1:T(8,128)(2,1)S(1)}, bf16[128,2,462]{0,2,1:T(8,128)(2,1)S(1)}, u32[]{:S(2)}, u32[]{:S(2)}) collective-permute-start(bf16[128,2,462]{0,2,1:T(8,128)(2,1)S(1)} %collective-permute-done.38), channel_id=1, source_target_pairs={{0,32},{32,64},{64,96},{96,128},{128,160},{160,192},{192,224},{224... | collective-permute-start | bytes 709640 | tf_op jit(solution)/shard_map/ppermute | solution.py:48
  153.1 43.2 %copy-start.17 = (bf16[128,462]{0,1:T(8,128)(2,1)}, bf16[128,462]{0,1:T(8,128)(2,1)S(1)}, u32[]{:S(2)}) copy-start(bf16[128,462]{0,1:T(8,128)(2,1)S(1)} %collective-permute-done.16) | copy-start | bytes 354820
  153.1 7.5 %collective-permute-start.18 = (bf16[128,462]{0,1:T(8,128)(2,1)S(1)}, bf16[128,462]{0,1:T(8,128)(2,1)S(1)}, u32[]{:S(2)}, u32[]{:S(2)}) collective-permute-start(bf16[128,462]{0,1:T(8,128)(2,1)S(1)} %collective-permute-done.16), channel_id=1, source_target_pairs={{0,480},{32,0},{64,32},{96,64},{128,96},{160,128},{192,160},{224,1... | collective-permute-start | bytes 354824 | tf_op jit(solution)/shard_map/ppermute | solution.py:51
  158.3 58.3 %copy-start.13 = (bf16[128,462]{0,1:T(8,128)(2,1)}, bf16[128,462]{0,1:T(8,128)(2,1)S(1)}, u32[]{:S(2)}) copy-start(bf16[128,462]{0,1:T(8,128)(2,1)S(1)} %collective-permute-done.17) | copy-start | bytes 354820
  158.3 7.9 %collective-permute-start.19 = (bf16[128,462]{0,1:T(8,128)(2,1)S(1)}, bf16[128,462]{0,1:T(8,128)(2,1)S(1)}, u32[]{:S(2)}, u32[]{:S(2)}) collective-permute-start(bf16[128,462]{0,1:T(8,128)(2,1)S(1)} %collective-permute-done.17), channel_id=1, source_target_pairs={{0,32},{32,64},{64,96},{96,128},{128,160},{160,192},{192,224},{224... | collective-permute-start | bytes 354824 | tf_op jit(solution)/shard_map/ppermute | solution.py:48
  160.6 42.8 %copy-start.23 = (bf16[128,462]{0,1:T(8,128)(2,1)}, bf16[128,462]{0,1:T(8,128)(2,1)S(1)}, u32[]{:S(2)}) copy-start(bf16[128,462]{0,1:T(8,128)(2,1)S(1)} %collective-permute-done.18) | copy-start | bytes 354820
  160.6 14.6 %collective-permute-start.20 = (bf16[128,462]{0,1:T(8,128)(2,1)S(1)}, bf16[128,462]{0,1:T(8,128)(2,1)S(1)}, u32[]{:S(2)}, u32[]{:S(2)}) collective-permute-start(bf16[128,462]{0,1:T(8,128)(2,1)S(1)} %collective-permute-done.18), channel_id=1, source_target_pairs={{0,480},{32,0},{64,32},{96,64},{128,96},{160,128},{192,160},{224,1... | collective-permute-start | bytes 354824 | tf_op jit(solution)/shard_map/ppermute | solution.py:51
  166.2 32.0 %copy-start.19 = (bf16[128,462]{0,1:T(8,128)(2,1)}, bf16[128,462]{0,1:T(8,128)(2,1)S(1)}, u32[]{:S(2)}) copy-start(bf16[128,462]{0,1:T(8,128)(2,1)S(1)} %collective-permute-done.19) | copy-start | bytes 354820
  166.2 14.2 %collective-permute-start.21 = (bf16[128,462]{0,1:T(8,128)(2,1)S(1)}, bf16[128,462]{0,1:T(8,128)(2,1)S(1)}, u32[]{:S(2)}, u32[]{:S(2)}) collective-permute-start(bf16[128,462]{0,1:T(8,128)(2,1)S(1)} %collective-permute-done.19), channel_id=1, source_target_pairs={{0,32},{32,64},{64,96},{96,128},{128,160},{160,192},{192,224},{224... | collective-permute-start | bytes 354824 | tf_op jit(solution)/shard_map/ppermute | solution.py:48
  168.2 23.0 %collective-permute-start.41 = (bf16[128,2,462]{0,2,1:T(8,128)(2,1)S(1)}, bf16[128,2,462]{0,2,1:T(8,128)(2,1)S(1)}, u32[]{:S(2)}, u32[]{:S(2)}) collective-permute-start(bf16[128,2,462]{0,2,1:T(8,128)(2,1)S(1)} %collective-permute-done.39), channel_id=1, source_target_pairs={{0,480},{32,0},{64,32},{96,64},{128,96},{160,128},{192,160},{224,1... | collective-permute-start | bytes 709640 | tf_op jit(solution)/shard_map/ppermute | solution.py:51
  173.3 23.0 %collective-permute-start.42 = (bf16[128,2,462]{0,2,1:T(8,128)(2,1)S(1)}, bf16[128,2,462]{0,2,1:T(8,128)(2,1)S(1)}, u32[]{:S(2)}, u32[]{:S(2)}) collective-permute-start(bf16[128,2,462]{0,2,1:T(8,128)(2,1)S(1)} %collective-permute-done.40), channel_id=1, source_target_pairs={{0,32},{32,64},{64,96},{96,128},{128,160},{160,192},{192,224},{224... | collective-permute-start | bytes 709640 | tf_op jit(solution)/shard_map/ppermute | solution.py:48
  175.3 8.1 %collective-permute-start.22 = (bf16[128,462]{0,1:T(8,128)(2,1)S(1)}, bf16[128,462]{0,1:T(8,128)(2,1)S(1)}, u32[]{:S(2)}, u32[]{:S(2)}) collective-permute-start(bf16[128,462]{0,1:T(8,128)(2,1)S(1)} %collective-permute-done.20), channel_id=1, source_target_pairs={{0,480},{32,0},{64,32},{96,64},{128,96},{160,128},{192,160},{224,1... | collective-permute-start | bytes 354824 | tf_op jit(solution)/shard_map/ppermute | solution.py:51
  180.4 8.8 %collective-permute-start.23 = (bf16[128,462]{0,1:T(8,128)(2,1)S(1)}, bf16[128,462]{0,1:T(8,128)(2,1)S(1)}, u32[]{:S(2)}, u32[]{:S(2)}) collective-permute-start(bf16[128,462]{0,1:T(8,128)(2,1)S(1)} %collective-permute-done.21), channel_id=1, source_target_pairs={{0,32},{32,64},{64,96},{96,128},{128,160},{160,192},{192,224},{224... | collective-permute-start | bytes 354824 | tf_op jit(solution)/shard_map/ppermute | solution.py:48
  183.3 14.9 %collective-permute-start.24 = (bf16[128,462]{0,1:T(8,128)(2,1)S(1)}, bf16[128,462]{0,1:T(8,128)(2,1)S(1)}, u32[]{:S(2)}, u32[]{:S(2)}) collective-permute-start(bf16[128,462]{0,1:T(8,128)(2,1)S(1)} %collective-permute-done.22), channel_id=1, source_target_pairs={{0,480},{32,0},{64,32},{96,64},{128,96},{160,128},{192,160},{224,1... | collective-permute-start | bytes 354824 | tf_op jit(solution)/shard_map/ppermute | solution.py:51
  189.2 14.2 %collective-permute-start.25 = (bf16[128,462]{0,1:T(8,128)(2,1)S(1)}, bf16[128,462]{0,1:T(8,128)(2,1)S(1)}, u32[]{:S(2)}, u32[]{:S(2)}) collective-permute-start(bf16[128,462]{0,1:T(8,128)(2,1)S(1)} %collective-permute-done.23), channel_id=1, source_target_pairs={{0,32},{32,64},{64,96},{96,128},{128,160},{160,192},{192,224},{224... | collective-permute-start | bytes 354824 | tf_op jit(solution)/shard_map/ppermute | solution.py:48
  191.2 220.2 %collective-permute-start.43 = (bf16[128,2,462]{0,2,1:T(8,128)(2,1)S(1)}, bf16[128,2,462]{0,2,1:T(8,128)(2,1)}, u32[]{:S(2)}, u32[]{:S(2)}) collective-permute-start(bf16[128,2,462]{0,2,1:T(8,128)(2,1)S(1)} %collective-permute-done.41), channel_id=1, source_target_pairs={{0,480},{32,0},{64,32},{96,64},{128,96},{160,128},{192,160},{224,1... | collective-permute-start | bytes 709640 | tf_op jit(solution)/shard_map/ppermute | solution.py:51
  196.3 244.9 %collective-permute-start.44 = (bf16[128,2,462]{0,2,1:T(8,128)(2,1)S(1)}, bf16[128,2,462]{0,2,1:T(8,128)(2,1)}, u32[]{:S(2)}, u32[]{:S(2)}) collective-permute-start(bf16[128,2,462]{0,2,1:T(8,128)(2,1)S(1)} %collective-permute-done.42), channel_id=1, source_target_pairs={{0,32},{32,64},{64,96},{96,128},{128,160},{160,192},{192,224},{224... | collective-permute-start | bytes 709640 | tf_op jit(solution)/shard_map/ppermute | solution.py:48
  198.3 7.5 %collective-permute-start.26 = (bf16[128,462]{0,1:T(8,128)(2,1)S(1)}, bf16[128,462]{0,1:T(8,128)(2,1)}, u32[]{:S(2)}, u32[]{:S(2)}) collective-permute-start(bf16[128,462]{0,1:T(8,128)(2,1)S(1)} %collective-permute-done.24), channel_id=1, source_target_pairs={{0,480},{32,0},{64,32},{96,64},{128,96},{160,128},{192,160},{224,1... | collective-permute-start | bytes 354824 | tf_op jit(solution)/shard_map/ppermute | solution.py:51
  203.5 8.0 %collective-permute-start.27 = (bf16[128,462]{0,1:T(8,128)(2,1)S(1)}, bf16[128,462]{0,1:T(8,128)(2,1)}, u32[]{:S(2)}, u32[]{:S(2)}) collective-permute-start(bf16[128,462]{0,1:T(8,128)(2,1)S(1)} %collective-permute-done.25), channel_id=1, source_target_pairs={{0,32},{32,64},{64,96},{96,128},{128,160},{160,192},{192,224},{224... | collective-permute-start | bytes 354824 | tf_op jit(solution)/shard_map/ppermute | solution.py:48
  205.8 340.9 %collective-permute-start.28 = (bf16[128,462]{0,1:T(8,128)(2,1)}, bf16[128,462]{0,1:T(8,128)(2,1)}, u32[]{:S(2)}, u32[]{:S(2)}) collective-permute-start(bf16[128,462]{0,1:T(8,128)(2,1)} %collective-permute-done.26), channel_id=1, source_target_pairs={{0,480},{32,0},{64,32},{96,64},{128,96},{160,128},{192,160},{224,1... | collective-permute-start | bytes 354824 | tf_op jit(solution)/shard_map/ppermute | solution.py:51
  211.5 348.6 %collective-permute-start.29 = (bf16[128,462]{0,1:T(8,128)(2,1)}, bf16[128,462]{0,1:T(8,128)(2,1)}, u32[]{:S(2)}, u32[]{:S(2)}) collective-permute-start(bf16[128,462]{0,1:T(8,128)(2,1)} %collective-permute-done.27), channel_id=1, source_target_pairs={{0,32},{32,64},{64,96},{96,128},{128,160},{160,192},{192,224},{224... | collective-permute-start | bytes 354824 | tf_op jit(solution)/shard_map/ppermute | solution.py:48
  261.2 32.6 %copy-start.12 = (bf16[128,2,462]{0,2,1:T(8,128)(2,1)S(1)}, bf16[128,2,462]{0,2,1:T(8,128)(2,1)}, u32[]{:S(2)}) copy-start(bf16[128,2,462]{0,2,1:T(8,128)(2,1)} %copy-done.11) | copy-start | bytes 709636
  278.2 44.6 %copy-start.10 = (bf16[128,2,462]{0,2,1:T(8,128)(2,1)S(1)}, bf16[128,2,462]{0,2,1:T(8,128)(2,1)}, u32[]{:S(2)}) copy-start(bf16[128,2,462]{0,2,1:T(8,128)(2,1)} %copy-done.9) | copy-start | bytes 709636
  461.8 31.7 %copy-start.20 = (bf16[128,462]{0,1:T(8,128)(2,1)S(1)}, bf16[128,462]{0,1:T(8,128)(2,1)}, u32[]{:S(2)}) copy-start(bf16[128,462]{0,1:T(8,128)(2,1)} %copy-done.19) | copy-start | bytes 354820
  461.8 31.8 %copy-start.26 = (bf16[128,462]{0,1:T(8,128)(2,1)S(1)}, bf16[128,462]{0,1:T(8,128)(2,1)}, u32[]{:S(2)}) copy-start(bf16[128,462]{0,1:T(8,128)(2,1)} %copy-done.25) | copy-start | bytes 354820
  468.4 37.8 %copy-start.22 = (bf16[128,462]{0,1:T(8,128)(2,1)S(1)}, bf16[128,462]{0,1:T(8,128)(2,1)}, u32[]{:S(2)}) copy-start(bf16[128,462]{0,1:T(8,128)(2,1)} %copy-done.21) | copy-start | bytes 354820
  474.5 31.8 %copy-start.32 = (bf16[128,462]{0,1:T(8,128)(2,1)S(1)}, bf16[128,462]{0,1:T(8,128)(2,1)}, u32[]{:S(2)}) copy-start(bf16[128,462]{0,1:T(8,128)(2,1)} %copy-done.31) | copy-start | bytes 354820
  481.1 38.2 %copy-start.28 = (bf16[128,462]{0,1:T(8,128)(2,1)S(1)}, bf16[128,462]{0,1:T(8,128)(2,1)}, u32[]{:S(2)}) copy-start(bf16[128,462]{0,1:T(8,128)(2,1)} %copy-done.27) | copy-start | bytes 354820
  487.3 32.2 %copy-start.34 = (bf16[128,462]{0,1:T(8,128)(2,1)S(1)}, bf16[128,462]{0,1:T(8,128)(2,1)}, u32[]{:S(2)}) copy-start(bf16[128,462]{0,1:T(8,128)(2,1)} %copy-done.33) | copy-start | bytes 354820
  493.9 38.2 %copy-start.30 = (bf16[128,462]{0,1:T(8,128)(2,1)S(1)}, bf16[128,462]{0,1:T(8,128)(2,1)}, u32[]{:S(2)}) copy-start(bf16[128,462]{0,1:T(8,128)(2,1)} %copy-done.29) | copy-start | bytes 354820
  (22 other events, 276.0 us)
Sparse Core Ops, SparseCore 0:
  57.8 59.4 all-gather.1
  576.5 98.1 reduce-scatter.1
